TPU v7x, 128 devices: a whole 4x4x4 slice. The times are simulated.
128 devices in a mesh: ord: 16 (over x, y_lo, core), lat: 8 (over z, y_hi).
Axes of the slice: x: 4, y: 4 (y_hi: 2, y_lo: 2; y = y_hi * 2 + y_lo), z: 4, core: 2. Of those that a mesh axis runs over, the one named last changes fastest.
Arguments:
- grad_coef: bfloat16 [768, 768, 256], P(('ord', 'lat')), may hold values from -6 to 6
- legendre: bfloat16 [768, 256, 768], P('ord', 'lat'), may hold values from -0.0078125 to 0.0078125
- quad_weight: float32 [256], P('lat'), may hold values from 0.3 to 1
- slot_order: int32 [768], replicated, may hold values from 0 to 767, as said below
- slot_count: int32 [768], P('ord'), may hold values from 0 to 721, as said below
- conv_input: bfloat16 [256, 128, 1440], P(('lat', 'ord')), may hold values from -6 to 6
- depth_kernel: float32 [128, 25], replicated, may hold values from -1.25 to 1.25
- point_weight: bfloat16 [128, 128], replicated, may hold values from -0.5 to 0.5
Outputs:
- grad_input: bfloat16 [256, 128, 1440], P(('lat', 'ord'))
- grad_point: float32 [128, 128], replicated
- grad_depth: float32 [128, 25], replicated
Inputs may be any that keep to these rules, and one draw needn't show every extreme that they name: `slot_order`: a permutation of 0 to 767; slots g*48 to (g+1)*48 - 1 hold the orders of one aligned block of 48 orders, in some order. `slot_count`: 721 minus the slot's order in slot_order, or 0 where that is negative.
All inputs are finite; a program needn't handle non-finite values.
Results may differ from a plain program's by a relative error of at most 0.0068.
Values may be sent and summed in bfloat16 or wider, within the bound.
No kernel may reach another device: no remote copies, remote signals or barrier semaphores. Data moves between devices by JAX's collectives and lax.ppermute only.
A program may use at most 192 MiB of HBM per device.

v0:
```python
import math

import jax
import jax.numpy as jnp
from jax import lax
from jax.sharding import PartitionSpec as P


MESH_AXES = ("ord", "lat")
WRAP = 8


def device_of_block(k):
    n_ord, n_lat = lax.axis_size("ord"), lax.axis_size("lat")
    l, o = divmod(k, n_ord)
    return o * n_lat + l


def with_rims(field, width=2):
    count = lax.axis_size("ord") * lax.axis_size("lat")
    down_pairs = [(device_of_block(k), device_of_block(k + 1)) for k in range(count - 1)]
    up_pairs = [(device_of_block(k + 1), device_of_block(k)) for k in range(count - 1)]
    upper = lax.ppermute(field[field.shape[0] - width :], MESH_AXES, down_pairs)
    lower = lax.ppermute(field[:width], MESH_AXES, up_pairs)
    return jnp.concatenate([upper, field, lower], axis=0)


def group_sum(value, bits):
    count = lax.axis_size("ord") * lax.axis_size("lat")
    me = lax.axis_index("ord") * lax.axis_size("lat") + lax.axis_index("lat")
    size = 1 << len(bits)

    def mask_of(x):
        return sum(((x >> i) & 1) << bit for i, bit in enumerate(bits))

    held = [value]
    for x in range(1, size):
        mask = mask_of(x)
        held.append(lax.ppermute(value, MESH_AXES, [(d, d ^ mask) for d in range(count)]))
    held = jnp.stack(held)
    position = sum(((me >> bit) & 1) << i for i, bit in enumerate(bits))
    members = [lax.dynamic_index_in_dim(held, position ^ j, keepdims=False) for j in range(size)]
    while len(members) > 1:
        members = [members[i] + members[i + 1] for i in range(0, len(members), 2)]
    return members[0]


def butterfly_sum(value, carry, steps):
    count = lax.axis_size("ord") * lax.axis_size("lat")
    bits = list(range(count.bit_length() - 1))
    preferred = [(3, 4), (1, 2), (5, 6), (0,)]
    rounds = [tuple(b for b in group if b in bits) for group in preferred]
    rounds = [group for group in rounds if group]
    left = [b for b in bits if all(b not in group for group in rounds)]
    rounds += [(b,) for b in left]
    for round_index, group in enumerate(rounds):
        if round_index < len(steps):
            carry = steps[round_index](carry)
        value, carry = lax.optimization_barrier((group_sum(value, group), carry))
    for step in steps[len(rounds):]:
        carry = step(carry)
    return value, carry


def wrap_longitudes(field, width):
    return jnp.concatenate([field[:, -width:], field, field[:, :width]], axis=1)


def make_table(orders, length, outer):
    inner = length // outer
    step = 2.0 * math.pi / length
    m = orders[None, None, :]
    coarse = jnp.arange(outer, dtype=jnp.int32)[:, None, None]
    fine = jnp.arange(inner, dtype=jnp.int32)[None, :, None]
    angle_a = ((m * inner * coarse) % length).astype(jnp.float32) * step
    angle_b = ((m * fine) % length).astype(jnp.float32) * step
    cos_a, sin_a = jnp.cos(angle_a), jnp.sin(angle_a)
    cos_b, sin_b = jnp.cos(angle_b), jnp.sin(angle_b)
    cosine = cos_a * cos_b - sin_a * sin_b
    sine = sin_a * cos_b + cos_a * sin_b
    factor = jnp.where((orders == 0) | (2 * orders == length), 1.0, 2.0).astype(jnp.float32)
    parts = jnp.stack([factor * cosine, -factor * sine]).astype(jnp.bfloat16)
    return parts.reshape(2 * length, orders.shape[0])


def layer(
    grad_coef, legendre, quad_weight, slot_order, slot_count, conv_input, depth_kernel, point_weight
):
    n_ord = lax.axis_size("ord")
    n_lat = lax.axis_size("lat")
    own_slots, degrees, doubled = grad_coef.shape
    row_count, channels, longitudes = conv_input.shape
    lat_index = lax.axis_index("lat")

    x_rows = with_rims(conv_input.transpose(0, 2, 1))
    x_pad = wrap_longitudes(x_rows.astype(jnp.float32), WRAP)

    _, band_rows, _ = legendre.shape
    pieces = []
    rest = quad_weight
    for _ in range(4):
        piece = lax.reduce_precision(rest, exponent_bits=8, mantissa_bits=7)
        pieces.append(piece.astype(jnp.bfloat16))
        rest = rest - piece
    extra = jnp.concatenate(pieces)
    extra = jnp.pad(extra, (0, degrees - extra.shape[0]))
    extra = jnp.broadcast_to(extra, (n_lat, 8, degrees))
    chunks = legendre.reshape(n_lat, own_slots * band_rows, degrees)
    payload = jnp.concatenate([chunks, extra.astype(legendre.dtype)], axis=1)
    arrived = lax.all_to_all(payload, "lat", 0, 0, tiled=True)
    hidden = jnp.zeros((row_count, longitudes, channels), jnp.float32)
    for tap_row in range(5):
        for tap_col in range(5):
            weight_tap = depth_kernel[:, 5 * tap_row + tap_col]
            start = WRAP - 2 + tap_col
            hidden = hidden + weight_tap * x_pad[
                tap_row : tap_row + row_count, start : start + longitudes
            ]
    hidden = hidden.astype(jnp.bfloat16)
    counts = lax.dynamic_slice_in_dim(slot_count, lat_index * own_slots, own_slots)
    is_valid = jnp.arange(degrees, dtype=jnp.int32)[None, :] < counts[:, None]
    masked = grad_coef * is_valid[:, :, None].astype(grad_coef.dtype)
    source = jnp.arange(doubled, dtype=jnp.int32)
    target = (source % 2) * channels + source // 2
    permute = (target[:, None] == source[None, :]).astype(grad_coef.dtype)
    masked = jnp.einsum("sjk,kt->sjt", masked, permute, preferred_element_type=jnp.float32)
    masked = masked.astype(grad_coef.dtype)
    arrived, hidden, masked = lax.optimization_barrier((arrived, hidden, masked))
    body = arrived[:, : own_slots * band_rows].reshape(n_lat, own_slots, band_rows, degrees)
    leg_rows = body.transpose(1, 0, 2, 3).reshape(own_slots, n_lat * band_rows, degrees)
    parts = arrived[:, own_slots * band_rows, : 4 * band_rows].astype(jnp.float32)
    parts = parts.reshape(n_lat, 4, band_rows)
    weights = ((parts[:, 3] + parts[:, 2]) + parts[:, 1]) + parts[:, 0]
    weights = weights.reshape(-1)
    summed = jnp.einsum("slj,sjk->slk", leg_rows, masked, preferred_element_type=jnp.float32)
    spectral = (summed * weights[None, :, None]).astype(jnp.bfloat16)
    by_device = spectral.reshape(own_slots, n_lat, n_ord, row_count * doubled)
    by_device = by_device.transpose(0, 2, 1, 3).reshape(own_slots, n_ord * n_lat, -1)
    own_rows = lax.all_to_all(by_device, MESH_AXES, 1, 0, tiled=True)
    own_rows = own_rows.reshape(-1, row_count * doubled)

    table = make_table(slot_order, longitudes, 36 if longitudes % 36 == 0 else 1)
    per_row = own_rows.reshape(-1, row_count, doubled)
    grid_rows = []
    for row in range(row_count):
        both = jnp.einsum("qs,sn->qn", table, per_row[:, row], preferred_element_type=jnp.float32)
        grid_rows.append(both[:longitudes, :channels] + both[longitudes:, channels:])
    grad_grid = jnp.stack(grid_rows).astype(jnp.bfloat16)

    grad_hidden = jnp.einsum(
        "rqd,cd->rqc", grad_grid, point_weight, preferred_element_type=jnp.float32
    ).astype(jnp.bfloat16)
    point_part = jnp.einsum("rqc,rqd->cd", hidden, grad_grid, preferred_element_type=jnp.float32)
    hidden_wide = grad_hidden.astype(jnp.float32)
    depth_terms = []
    for tap_row in range(5):
        for tap_col in range(5):
            start = WRAP - 2 + tap_col
            shifted_x = x_pad[tap_row : tap_row + row_count, start : start + longitudes]
            depth_terms.append(jnp.sum(hidden_wide * shifted_x, axis=(0, 1)))
    depth_part = jnp.stack(depth_terms, axis=1)
    grad_pad = wrap_longitudes(with_rims(grad_hidden).astype(jnp.float32), WRAP)
    taps = [(tap_row, tap_col) for tap_row in range(5) for tap_col in range(5)]
    rounds = 4
    groups = [taps[i * len(taps) // rounds : (i + 1) * len(taps) // rounds] for i in range(rounds)]

    def tap_group(group):
        def step(grad_input):
            for tap_row, tap_col in group:
                weight_tap = depth_kernel[:, 5 * tap_row + tap_col]
                start = WRAP + 2 - tap_col
                grad_input = grad_input + weight_tap * grad_pad[
                    4 - tap_row : 4 - tap_row + row_count, start : start + longitudes
                ]
            return grad_input

        return step

    grad_input = jnp.zeros((row_count, longitudes, channels), jnp.float32)
    sums, grad_input = butterfly_sum(
        jnp.concatenate([point_part, depth_part], axis=1),
        grad_input,
        [tap_group(group) for group in groups],
    )
    grad_input = grad_input.astype(jnp.bfloat16).transpose(0, 2, 1)
    total_rows = row_count * n_ord * n_lat
    grad_scale = 1.0 / math.sqrt(total_rows * longitudes)
    sums = sums * grad_scale
    return (grad_input, sums[:, :channels], sums[:, channels:])


def solution(mesh):
    return jax.shard_map(
        layer,
        mesh=mesh,
        in_specs=(
            P(("ord", "lat"), None, None),
            P("ord", "lat", None),
            P("lat"),
            P(),
            P("ord"),
            P(("lat", "ord"), None, None),
            P(),
            P(),
        ),
        out_specs=(P(("lat", "ord"), None, None), P(), P()),
        check_vma=False,
    )
```

profile of v0, /device:TPU:1, one launch (start us, length us, event | category | flops | bytes accessed | tf_op | source)
XLA Modules:
  0.0 144.1 jit_solution(7508027668740142441)
XLA Ops:
  0.6 4.6 %collective-permute-start = (bf16[2,1440,128]{2,1,0:T(8,128)(2,1)}, bf16[2,1440,128]{2,1,0:T(8,128)(2,1)S(1)}, u32[]{:S(2)}, u32[]{:S(2)}) collective-permute-start(bf16[2,1440,128]{2,1,0:T(8,128)(2,1)} %bitcast.151), channel_id=1, source_target_pairs={{0,8},{8,16},{16,24},{24,32},{32,40},{40,48},{48,56},{56,64},{64,7... | collective-permute-start | bytes 2211848 | tf_op jit(solution)/shard_map/ppermute | solution.py:23
  5.2 1.9 %collective-permute-start.1 = (bf16[2,1440,128]{2,1,0:T(8,128)(2,1)}, bf16[2,1440,128]{2,1,0:T(8,128)(2,1)}, u32[]{:S(2)}, u32[]{:S(2)}) collective-permute-start(bf16[2,1440,128]{2,1,0:T(8,128)(2,1)} %bitcast.152), channel_id=1, source_target_pairs={{8,0},{16,8},{24,16},{32,24},{40,32},{48,40},{56,48},{64,56},{72,6... | collective-permute-start | bytes 2211848 | tf_op jit(solution)/shard_map/ppermute | solution.py:24
  7.2 0.7 reduce-precision_convert_fusion.2
  7.9 3.3 %pad_maximum_fusion.1 = bf16[8,200,768]{2,1,0:T(8,128)(2,1)} fusion(bf16[8,8,768]{2,1,0:T(8,128)(2,1)S(1)} %broadcast_in_dim.8, bf16[8,192,768]{2,1,0:T(8,128)(2,1)} %bitcast.149), kind=kLoop, calls=%fused_computation.65 | loop fusion | flops 4915200 | bytes 4915200 | tf_op jit(solution)/shard_map/concatenate | solution.py:109
  11.2 7.5 %all-to-all-start = ((bf16[8,200,768]{2,1,0:T(8,128)(2,1)}), bf16[8,200,768]{2,1,0:T(8,128)(2,1)S(1)}, u32[]{:S(2)}, u32[]{:S(2)}) async-start(bf16[8,200,768]{2,1,0:T(8,128)(2,1)} %pad_maximum_fusion.1), calls=%async_computation | async-start | bytes 4915200 | tf_op jit(solution)/shard_map/all_to_all | solution.py:110
  19.3 0.6 slice_bitcast_fusion.24
  20.1 1.3 fusion.135
  21.4 4.1 %fusion.2 = bf16[6,768,256]{2,1,0:T(8,128)(2,1)} fusion(bf16[6,768,256]{2,1,0:T(8,128)(2,1)} %param.8, bf16[6,768]{1,0:T(8,128)(2,1)S(1)} %fusion.143, s32[256]{0:T(256)S(1)} %fusion.157), kind=kOutput, calls=%fused_computation.106 | convolution fusion | flops 606404608 | bytes 4728832 | tf_op jit(solution)/shard_map/sjk,kt->sjt/dot_general | solution.py:126
  25.5 1.4 maximum_convert_fusion
  27.0 2.0 %copy-done.1 = f32[6,1440,128]{2,1,0:T(8,128)} copy-done((f32[6,1440,128]{2,1,0:T(8,128)}, f32[6,1440,128]{2,1,0:T(8,128)S(1)}, u32[]{:S(2)}) %copy-start.1) | copy-done | bytes 4423704
  29.0 7.6 %add_convert_fusion = (bf16[2,1440,128]{2,1,0:T(8,128)(2,1)}, f32[2,1440,128]{2,1,0:T(8,128)}, f32[2,1440,128]{2,1,0:T(8,128)}) fusion(f32[6,1440,128]{2,1,0:T(8,128)S(1)} %maximum_convert_fusion, f32[128]{0:T(128)S(1)} %get-tuple-element.98, f32[128]{0:T(128)S(1)} %get-tuple-element.99, f32[128]{0:T(128)S(1)} %get-tuple-element.76, ...), kind=kLoop, calls=%fused_computation.222 | loop fusion | flops 25804800 | bytes 15544832 | tf_op jit(solution)/shard_map/convert_element_type | solution.py:119
  36.6 18.1 %all-to-all-done = bf16[8,200,768]{2,1,0:T(8,128)(2,1)S(1)} async-done(((bf16[8,200,768]{2,1,0:T(8,128)(2,1)}), bf16[8,200,768]{2,1,0:T(8,128)(2,1)S(1)}, u32[]{:S(2)}, u32[]{:S(2)}) %all-to-all-start) | async-done | bytes 2457632 | tf_op jit(solution)/shard_map/all_to_all | solution.py:110
  55.3 2.4 %multiply_convert_fusion.2 = bf16[6,256,256]{2,1,0:T(8,128)(2,1)S(1)} fusion(bf16[6,256,768]{2,1,0:T(8,128)(2,1)S(1)} %bitcast.150, bf16[6,768,256]{2,1,0:T(8,128)(2,1)} %fusion.2, f32[256]{0:T(256)S(1)} %add.381), kind=kOutput, calls=%fused_computation.107 | convolution fusion | flops 604766208 | bytes 5506048 | tf_op jit(solution)/shard_map/slj,sjk->slk/dot_general | solution.py:135
  58.5 1.5 %copy.18 = bf16[6,128,512]{2,0,1:T(8,128)(2,1)} copy(bf16[6,128,512]{2,1,0:T(8,128)(2,1)S(1)} %bitcast.148) | data formatting | bytes 1572864 | tf_op jit(solution)/shard_map/reshape | solution.py:138
  59.9 5.1 %all-to-all-start.1 = ((bf16[6,128,512]{2,0,1:T(8,128)(2,1)}), bf16[6,128,512]{2,0,1:T(8,128)(2,1)S(1)}, u32[]{:S(2)}, u32[]{:S(2)}) async-start(bf16[6,128,512]{2,0,1:T(8,128)(2,1)} %copy.18), calls=%async_computation.1 | async-start | bytes 2097152 | tf_op jit(solution)/shard_map/all_to_all | solution.py:139
  65.0 1.6 %multiply_convert_fusion.1 = (bf16[1,36,40,768]{3,2,1,0:T(8,128)(2,1)S(1)}, bf16[1,36,40,768]{3,2,1,0:T(8,128)(2,1)S(1)}) fusion(f32[40,768]{1,0:T(8,128)S(1)} %get-tuple-element.105, f32[36,768]{1,0:T(8,128)S(1)} %copy-done.8, f32[40,768]{1,0:T(8,128)S(1)} %get-tuple-element.104, f32[36,768]{1,0:T(8,128)S(1)} %copy-done.7, f32[768]{0:T(1024)S(1)} %get-tuple-element.100, ...), kind=kLoop, calls=%fused_computation.63 | loop fusion | flops 11059200 | bytes 4896768 | tf_op jit(solution)/shard_map/convert.5
  66.6 2.5 %pad_maximum_fusion = bf16[2,36,40,768]{3,2,1,0:T(8,128)(2,1)} fusion(bf16[1,36,40,768]{3,2,1,0:T(8,128)(2,1)S(1)} %get-tuple-element.74, bf16[1,36,40,768]{3,2,1,0:T(8,128)(2,1)S(1)} %get-tuple-element.73), kind=kLoop, calls=%fused_computation.61 | loop fusion | flops 2211840 | bytes 8847360 | tf_op jit(solution)/shard_map/stack | solution.py:82
  69.1 15.4 %all-to-all-done.1 = bf16[6,128,512]{2,0,1:T(8,128)(2,1)S(1)} async-done(((bf16[6,128,512]{2,0,1:T(8,128)(2,1)}), bf16[6,128,512]{2,0,1:T(8,128)(2,1)S(1)}, u32[]{:S(2)}, u32[]{:S(2)}) %all-to-all-start.1) | async-done | bytes 786464 | tf_op jit(solution)/shard_map/all_to_all | solution.py:139
  84.9 1.1 fusion.165
  86.0 3.8 %fusion.113 = f32[2880,256]{1,0:T(8,128)S(1)} fusion(bf16[2880,768]{1,0:T(8,128)(2,1)} %bitcast.144, bf16[768,1,256]{2,1,0:T(2,128)(2,1)S(1)} %get-tuple-element.72), kind=kOutput, calls=%fused_computation.232 | convolution fusion | flops 1132462080 | bytes 7766016 | tf_op jit(solution)/shard_map/qs,sn->qn/dot_general | solution.py:146
  89.8 1.3 fusion.116
  91.3 2.4 %fusion.102 = (f32[128]{0:T(128)S(1)}, f32[128]{0:T(128)S(1)}, f32[128]{0:T(128)S(1)}, f32[128]{0:T(128)S(1)}, f32[128]{0:T(128)S(1)}, /*index=5*/f32[128]{0:T(1...) fusion(f32[6,1440,128]{2,1,0:T(8,128)S(1)} %bitcast.143, ...), kind=kOutput, calls=%fused_computation.205 | convolution fusion | flops 105429888 | bytes 5960192 | tf_op jit(solution)/shard_map/rqd,cd->rqc/dot_general | solution.py:150
  93.8 2.1 %collective-permute-start.5 = (bf16[2,1440,128]{2,1,0:T(8,128)(2,1)S(1)}, bf16[2,1440,128]{2,1,0:T(8,128)(2,1)S(1)}, u32[]{:S(2)}, u32[]{:S(2)}) collective-permute-start(bf16[2,1440,128]{2,1,0:T(8,128)(2,1)S(1)} %get-tuple-element.110), channel_id=1, source_target_pairs={{0,8},{8,16},{16,24},{24,32},{32,40},{40,48},{48,56},{56,64},{64,7... | collective-permute-start | bytes 2211848 | tf_op jit(solution)/shard_map/ppermute | solution.py:23
  95.9 2.4 %collective-permute-start.6 = (bf16[2,1440,128]{2,1,0:T(8,128)(2,1)S(1)}, bf16[2,1440,128]{2,1,0:T(8,128)(2,1)S(1)}, u32[]{:S(2)}, u32[]{:S(2)}) collective-permute-start(bf16[2,1440,128]{2,1,0:T(8,128)(2,1)S(1)} %get-tuple-element.110), channel_id=1, source_target_pairs={{8,0},{16,8},{24,16},{32,24},{40,32},{48,40},{56,48},{64,56},{72,6... | collective-permute-start | bytes 2211848 | tf_op jit(solution)/shard_map/ppermute | solution.py:24
  98.3 3.4 %fusion.105 = (f32[128]{0:T(128)S(1)}, f32[128]{0:T(128)S(1)}, f32[128]{0:T(128)S(1)}, f32[128]{0:T(128)S(1)}, f32[128]{0:T(128)S(1)}, /*index=5*/f32[128]{0:T(1...) fusion(bf16[2,1440,128]{2,1,0:T(8,128)(2,1)S(1)} %get-tuple-element.110, f32[6,8,128]{2,1,0:T(8,128)S(1)} %get-tuple-element.69, ...), kind=kLoop, calls=%fused_computation.208 | loop fusion | flops 10320768 | bytes 5190144 | tf_op jit(solution)/shard_map/reduce_sum | solution.py:160
  102.2 0.9 copy-done.3
  103.1 0.8 fusion.106
  104.1 1.3 collective-permute-start.3
  105.4 0.8 collective-permute-start.4
  106.2 8.6 %collective-permute-done.3 = f32[128,153]{0,1:T(8,128)S(1)} collective-permute-done((f32[128,153]{0,1:T(8,128)S(1)}, f32[128,153]{0,1:T(8,128)S(1)}, u32[]{:S(2)}, u32[]{:S(2)}) %collective-permute-start.3) | collective-permute-done | bytes 78368 | tf_op jit(solution)/shard_map/ppermute | solution.py:39
  114.8 0.9 collective-permute-done.4
  116.4 1.2 fusion.13
  117.6 0.9 collective-permute-start.7
  118.5 2.3 %collective-permute-start.8 = (f32[128,153]{0,1:T(8,128)S(1)}, f32[128,153]{0,1:T(8,128)S(1)}, u32[]{:S(2)}, u32[]{:S(2)}) collective-permute-start(f32[128,153]{0,1:T(8,128)S(1)} %add_bitcast_fusion.2), channel_id=1, source_target_pairs={{0,4},{1,5},{2,6},{3,7},{4,0},{5,1},{6,2},{7,3},{8,12},{9,13},{10,... | collective-permute-start | bytes 235016 | tf_op jit(solution)/shard_map/ppermute | solution.py:39
  120.7 1.0 collective-permute-start.9
  121.8 1.3 fusion.21
  123.1 2.3 %collective-permute-done.8 = f32[128,153]{0,1:T(8,128)S(1)} collective-permute-done((f32[128,153]{0,1:T(8,128)S(1)}, f32[128,153]{0,1:T(8,128)S(1)}, u32[]{:S(2)}, u32[]{:S(2)}) %collective-permute-start.8) | collective-permute-done | bytes 78368 | tf_op jit(solution)/shard_map/ppermute | solution.py:39
  125.5 1.7 %collective-permute-done.9 = f32[128,153]{0,1:T(8,128)S(1)} collective-permute-done((f32[128,153]{0,1:T(8,128)S(1)}, f32[128,153]{0,1:T(8,128)S(1)}, u32[]{:S(2)}, u32[]{:S(2)}) %collective-permute-start.9) | collective-permute-done | bytes 78368 | tf_op jit(solution)/shard_map/ppermute | solution.py:39
  127.3 2.8 %collective-permute-start.10 = (f32[128,153]{0,1:T(8,128)S(1)}, f32[128,153]{0,1:T(8,128)S(1)}, u32[]{:S(2)}, u32[]{:S(2)}) collective-permute-start(f32[128,153]{0,1:T(8,128)S(1)} %add_bitcast_fusion.1), channel_id=1, source_target_pairs={{0,32},{1,33},{2,34},{3,35},{4,36},{5,37},{6,38},{7,39},{8,40},{9,... | collective-permute-start | bytes 235016 | tf_op jit(solution)/shard_map/ppermute | solution.py:39
  130.0 1.8 %collective-permute-start.11 = (f32[128,153]{0,1:T(8,128)S(1)}, f32[128,153]{0,1:T(8,128)S(1)}, u32[]{:S(2)}, u32[]{:S(2)}) collective-permute-start(f32[128,153]{0,1:T(8,128)S(1)} %add_bitcast_fusion.1), channel_id=1, source_target_pairs={{0,64},{1,65},{2,66},{3,67},{4,68},{5,69},{6,70},{7,71},{8,72},{9,... | collective-permute-start | bytes 235016 | tf_op jit(solution)/shard_map/ppermute | solution.py:39
  131.8 0.7 collective-permute-start.12
  132.5 1.1 fusion.30
  133.7 2.3 %collective-permute-done.11 = f32[128,153]{0,1:T(8,128)S(1)} collective-permute-done((f32[128,153]{0,1:T(8,128)S(1)}, f32[128,153]{0,1:T(8,128)S(1)}, u32[]{:S(2)}, u32[]{:S(2)}) %collective-permute-start.11) | collective-permute-done | bytes 78368 | tf_op jit(solution)/shard_map/ppermute | solution.py:39
  136.0 1.8 %collective-permute-done.12 = f32[128,153]{0,1:T(8,128)S(1)} collective-permute-done((f32[128,153]{0,1:T(8,128)S(1)}, f32[128,153]{0,1:T(8,128)S(1)}, u32[]{:S(2)}, u32[]{:S(2)}) %collective-permute-start.12) | collective-permute-done | bytes 78368 | tf_op jit(solution)/shard_map/ppermute | solution.py:39
  137.8 0.7 collective-permute-start.13
  138.5 2.6 %fusion.8 = bf16[2,1440,128]{2,1,0:T(8,128)(2,1)} fusion(f32[6,1440,128]{2,1,0:T(8,128)S(1)} %maximum_convert_fusion.1, f32[2,1440,128]{2,1,0:T(8,128)S(1)} %fusion.30, f32[6,8,128]{2,1,0:T(8,128)S(1)} %get-tuple-element.68, f32[6,8,128]{2,1,0:T(8,128)S(1)} %get-tuple-element.67, f32[128]{0:T(128)S(1)} %get-tuple-element.98, f32[128]{0:T(128)S(1)} %get-tuple-element.99, ...), kind=kLoop, calls=%fused_computation.111 | loop fusion | flops 7741440 | bytes 8162816 | tf_op jit(solution)/shard_map/add | solution.py:172
  141.2 1.5 %collective-permute-done.13 = f32[128,153]{0,1:T(8,128)S(1)} collective-permute-done((f32[128,153]{0,1:T(8,128)S(1)}, f32[128,153]{0,1:T(8,128)S(1)}, u32[]{:S(2)}, u32[]{:S(2)}) %collective-permute-start.13) | collective-permute-done | bytes 78368 | tf_op jit(solution)/shard_map/ppermute | solution.py:39
  143.4 0.7 copy.19
  (111 shorter events, 4.8 us)
Async XLA Ops:
  0.6 90.7 %copy-start = (bf16[128,128]{1,0:T(8,128)(2,1)S(1)}, bf16[128,128]{1,0:T(8,128)(2,1)}, u32[]{:S(2)}) copy-start(bf16[128,128]{1,0:T(8,128)(2,1)} %param.15) | copy-start | bytes 98308
  0.6 24.8 %collective-permute-start = (bf16[2,1440,128]{2,1,0:T(8,128)(2,1)}, bf16[2,1440,128]{2,1,0:T(8,128)(2,1)S(1)}, u32[]{:S(2)}, u32[]{:S(2)}) collective-permute-start(bf16[2,1440,128]{2,1,0:T(8,128)(2,1)} %bitcast.151), channel_id=1, source_target_pairs={{0,8},{8,16},{16,24},{24,32},{32,40},{40,48},{48,56},{56,64},{64,7... | collective-permute-start | bytes 2211848 | tf_op jit(solution)/shard_map/ppermute | solution.py:23
  5.2 20.3 %collective-permute-start.1 = (bf16[2,1440,128]{2,1,0:T(8,128)(2,1)}, bf16[2,1440,128]{2,1,0:T(8,128)(2,1)}, u32[]{:S(2)}, u32[]{:S(2)}) collective-permute-start(bf16[2,1440,128]{2,1,0:T(8,128)(2,1)} %bitcast.152), channel_id=1, source_target_pairs={{8,0},{16,8},{24,16},{32,24},{40,32},{48,40},{56,48},{64,56},{72,6... | collective-permute-start | bytes 2211848 | tf_op jit(solution)/shard_map/ppermute | solution.py:24
  11.2 7.5 %copy-start.9 = (s32[768]{0:T(1024)S(1)}, s32[768]{0:T(1024)}, u32[]{:S(2)}) copy-start(s32[768]{0:T(1024)} %param.11) | copy-start | bytes 9220
  11.2 8.1 %copy-start.10 = (f32[128,25]{0,1:T(8,128)S(1)}, f32[128,25]{0,1:T(8,128)}, u32[]{:S(2)}) copy-start(f32[128,25]{0,1:T(8,128)} %param.14) | copy-start | bytes 38404
  11.2 8.7 %copy-start.32 = (s32[48]{0:T(128)S(1)}, s32[48]{0:T(128)}, u32[]{:S(2)}) copy-start(s32[48]{0:T(128)} %param.12) | copy-start | bytes 580
  11.2 43.5 %all-to-all-start = ((bf16[8,200,768]{2,1,0:T(8,128)(2,1)}), bf16[8,200,768]{2,1,0:T(8,128)(2,1)S(1)}, u32[]{:S(2)}, u32[]{:S(2)}) async-start(bf16[8,200,768]{2,1,0:T(8,128)(2,1)} %pad_maximum_fusion.1), calls=%async_computation | async-start | bytes 4915200 | tf_op jit(solution)/shard_map/all_to_all | solution.py:110
  20.1 6.9 %copy-start.12 = (f32[128]{0:T(128)}, f32[128]{0:T(128)S(1)}, u32[]{:S(2)}) copy-start(f32[128]{0:T(128)S(1)} %get-tuple-element.94) | copy-start | bytes 1540
  20.1 6.9 %copy-start.14 = (f32[128]{0:T(128)}, f32[128]{0:T(128)S(1)}, u32[]{:S(2)}) copy-start(f32[128]{0:T(128)S(1)} %get-tuple-element.95) | copy-start | bytes 1540
  20.1 6.9 %copy-start.16 = (f32[128]{0:T(128)}, f32[128]{0:T(128)S(1)}, u32[]{:S(2)}) copy-start(f32[128]{0:T(128)S(1)} %get-tuple-element.96) | copy-start | bytes 1540
  20.1 6.9 %copy-start.18 = (f32[128]{0:T(128)}, f32[128]{0:T(128)S(1)}, u32[]{:S(2)}) copy-start(f32[128]{0:T(128)S(1)} %get-tuple-element.97) | copy-start | bytes 1540
  21.4 4.1 %copy-start.6 = (bf16[2,128,1440]{1,2,0:T(8,128)(2,1)S(1)}, bf16[2,128,1440]{1,2,0:T(8,128)(2,1)}, u32[]{:S(2)}) copy-start(bf16[2,128,1440]{1,2,0:T(8,128)(2,1)} %param.13) | copy-start | bytes 2211844
  25.4 3.5 %copy-start.11 = (f32[128]{0:T(128)S(1)}, f32[128]{0:T(128)}, u32[]{:S(2)}) copy-start(f32[128]{0:T(128)} %get-tuple-element.93) | copy-start | bytes 1540
  25.4 3.5 %copy-start.20 = (f32[128]{0:T(128)S(1)}, f32[128]{0:T(128)}, u32[]{:S(2)}) copy-start(f32[128]{0:T(128)} %get-tuple-element.87) | copy-start | bytes 1540
  25.4 3.5 %copy-start.22 = (f32[128]{0:T(128)S(1)}, f32[128]{0:T(128)}, u32[]{:S(2)}) copy-start(f32[128]{0:T(128)} %get-tuple-element.88) | copy-start | bytes 1540
  25.4 3.5 %copy-start.24 = (f32[128]{0:T(128)S(1)}, f32[128]{0:T(128)}, u32[]{:S(2)}) copy-start(f32[128]{0:T(128)} %get-tuple-element.89) | copy-start | bytes 1540
  25.5 3.5 %copy-start.26 = (f32[128]{0:T(128)S(1)}, f32[128]{0:T(128)}, u32[]{:S(2)}) copy-start(f32[128]{0:T(128)} %get-tuple-element.90) | copy-start | bytes 1540
  25.5 3.5 %copy-start.28 = (f32[128]{0:T(128)S(1)}, f32[128]{0:T(128)}, u32[]{:S(2)}) copy-start(f32[128]{0:T(128)} %get-tuple-element.91) | copy-start | bytes 1540
  25.5 3.5 %copy-start.30 = (f32[128]{0:T(128)S(1)}, f32[128]{0:T(128)}, u32[]{:S(2)}) copy-start(f32[128]{0:T(128)} %get-tuple-element.92) | copy-start | bytes 1540
  27.0 2.0 %copy-start.1 = (f32[6,1440,128]{2,1,0:T(8,128)}, f32[6,1440,128]{2,1,0:T(8,128)S(1)}, u32[]{:S(2)}) copy-start(f32[6,1440,128]{2,1,0:T(8,128)S(1)} %maximum_convert_fusion) | copy-start | bytes 13271044
  59.9 5.1 %copy-start.7 = (f32[36,768]{1,0:T(8,128)S(1)}, f32[36,768]{1,0:T(8,128)}, u32[]{:S(2)}) copy-start(f32[36,768]{1,0:T(8,128)} %get-tuple-element.102) | copy-start | bytes 331780
  59.9 5.1 %copy-start.8 = (f32[36,768]{1,0:T(8,128)S(1)}, f32[36,768]{1,0:T(8,128)}, u32[]{:S(2)}) copy-start(f32[36,768]{1,0:T(8,128)} %get-tuple-element.103) | copy-start | bytes 331780
  59.9 24.5 %all-to-all-start.1 = ((bf16[6,128,512]{2,0,1:T(8,128)(2,1)}), bf16[6,128,512]{2,0,1:T(8,128)(2,1)S(1)}, u32[]{:S(2)}, u32[]{:S(2)}) async-start(bf16[6,128,512]{2,0,1:T(8,128)(2,1)} %copy.18), calls=%async_computation.1 | async-start | bytes 2097152 | tf_op jit(solution)/shard_map/all_to_all | solution.py:139
  86.0 3.8 %copy-start.2 = (bf16[2,36,40,768]{3,2,1,0:T(8,128)(2,1)S(1)}, bf16[2,36,40,768]{3,2,1,0:T(8,128)(2,1)}, u32[]{:S(2)}) copy-start(bf16[2,36,40,768]{3,2,1,0:T(8,128)(2,1)} %pad_maximum_fusion) | copy-start | bytes 13271044
  86.0 5.3 %slice-start = ((s8[4423680]{0:T(1024)(128)(4,1)}), s8[4194304]{0:T(1024)(128)(4,1)S(1)}, s32[]{:S(2)}) async-start(s8[4423680]{0:T(1024)(128)(4,1)} %bitcast.142), calls=%async_computation.2 | async-start | bytes 8388608
  89.8 1.5 %slice-start.1 = ((s8[4423680]{0:T(1024)(128)(4,1)}), s8[229376]{0:T(1024)(128)(4,1)S(1)}, s32[]{:S(2)}) async-start(s8[4423680]{0:T(1024)(128)(4,1)} %bitcast.142), calls=%async_computation.3 | async-start | bytes 458752
  93.8 8.0 %copy-start.5 = (bf16[2,1440,128]{2,1,0:T(8,128)(2,1)S(1)}, bf16[2,1440,128]{2,1,0:T(8,128)(2,1)}, u32[]{:S(2)}) copy-start(bf16[2,1440,128]{2,1,0:T(8,128)(2,1)} %get-tuple-element.14) | copy-start | bytes 2211844
  93.8 22.0 %collective-permute-start.5 = (bf16[2,1440,128]{2,1,0:T(8,128)(2,1)S(1)}, bf16[2,1440,128]{2,1,0:T(8,128)(2,1)S(1)}, u32[]{:S(2)}, u32[]{:S(2)}) collective-permute-start(bf16[2,1440,128]{2,1,0:T(8,128)(2,1)S(1)} %get-tuple-element.110), channel_id=1, source_target_pairs={{0,8},{8,16},{16,24},{24,32},{32,40},{40,48},{48,56},{56,64},{64,7... | collective-permute-start | bytes 2211848 | tf_op jit(solution)/shard_map/ppermute | solution.py:23
  95.9 19.9 %collective-permute-start.6 = (bf16[2,1440,128]{2,1,0:T(8,128)(2,1)S(1)}, bf16[2,1440,128]{2,1,0:T(8,128)(2,1)S(1)}, u32[]{:S(2)}, u32[]{:S(2)}) collective-permute-start(bf16[2,1440,128]{2,1,0:T(8,128)(2,1)S(1)} %get-tuple-element.110), channel_id=1, source_target_pairs={{8,0},{16,8},{24,16},{32,24},{40,32},{48,40},{56,48},{64,56},{72,6... | collective-permute-start | bytes 2211848 | tf_op jit(solution)/shard_map/ppermute | solution.py:24
  98.3 3.9 %copy-start.4 = (f32[2,1440,128]{2,1,0:T(8,128)S(1)}, f32[2,1440,128]{2,1,0:T(8,128)}, u32[]{:S(2)}) copy-start(f32[2,1440,128]{2,1,0:T(8,128)} %get-tuple-element.66) | copy-start | bytes 4423684
  101.8 1.4 copy-start.3
  104.0 2.2 %collective-permute-start.2 = (f32[128,153]{0,1:T(8,128)S(1)}, f32[128,153]{0,1:T(8,128)S(1)}, u32[]{:S(2)}, u32[]{:S(2)}) collective-permute-start(f32[128,153]{0,1:T(8,128)S(1)} %concatenate.70), channel_id=1, source_target_pairs={{0,8},{1,9},{2,10},{3,11},{4,12},{5,13},{6,14},{7,15},{8,0},{9,1},... | collective-permute-start | bytes 235016 | tf_op jit(solution)/shard_map/ppermute | solution.py:39
  104.1 10.7 %collective-permute-start.3 = (f32[128,153]{0,1:T(8,128)S(1)}, f32[128,153]{0,1:T(8,128)S(1)}, u32[]{:S(2)}, u32[]{:S(2)}) collective-permute-start(f32[128,153]{0,1:T(8,128)S(1)} %concatenate.70), channel_id=1, source_target_pairs={{0,16},{1,17},{2,18},{3,19},{4,20},{5,21},{6,22},{7,23},{8,24},{9,... | collective-permute-start | bytes 235016 | tf_op jit(solution)/shard_map/ppermute | solution.py:39
  105.4 10.3 %collective-permute-start.4 = (f32[128,153]{0,1:T(8,128)S(1)}, f32[128,153]{0,1:T(8,128)S(1)}, u32[]{:S(2)}, u32[]{:S(2)}) collective-permute-start(f32[128,153]{0,1:T(8,128)S(1)} %concatenate.70), channel_id=1, source_target_pairs={{0,24},{1,25},{2,26},{3,27},{4,28},{5,29},{6,30},{7,31},{8,16},{9,... | collective-permute-start | bytes 235016 | tf_op jit(solution)/shard_map/ppermute | solution.py:39
  115.7 0.6 copy-start.17
  116.4 5.4 %copy-start.21 = (f32[128]{0:T(128)S(1)}, f32[128]{0:T(128)}, u32[]{:S(2)}) copy-start(f32[128]{0:T(128)} %get-tuple-element.87) | copy-start | bytes 1540
  116.4 5.4 %copy-start.23 = (f32[128]{0:T(128)S(1)}, f32[128]{0:T(128)}, u32[]{:S(2)}) copy-start(f32[128]{0:T(128)} %get-tuple-element.88) | copy-start | bytes 1540
  116.4 5.4 %copy-start.25 = (f32[128]{0:T(128)S(1)}, f32[128]{0:T(128)}, u32[]{:S(2)}) copy-start(f32[128]{0:T(128)} %get-tuple-element.89) | copy-start | bytes 1540
  116.4 5.4 %copy-start.27 = (f32[128]{0:T(128)S(1)}, f32[128]{0:T(128)}, u32[]{:S(2)}) copy-start(f32[128]{0:T(128)} %get-tuple-element.90) | copy-start | bytes 1540
  116.4 5.4 %copy-start.29 = (f32[128]{0:T(128)S(1)}, f32[128]{0:T(128)}, u32[]{:S(2)}) copy-start(f32[128]{0:T(128)} %get-tuple-element.91) | copy-start | bytes 1540
  116.4 5.4 %copy-start.31 = (f32[128]{0:T(128)S(1)}, f32[128]{0:T(128)}, u32[]{:S(2)}) copy-start(f32[128]{0:T(128)} %get-tuple-element.92) | copy-start | bytes 1540
  117.6 5.5 %collective-permute-start.7 = (f32[128,153]{0,1:T(8,128)S(1)}, f32[128,153]{0,1:T(8,128)S(1)}, u32[]{:S(2)}, u32[]{:S(2)}) collective-permute-start(f32[128,153]{0,1:T(8,128)S(1)} %add_bitcast_fusion.2), channel_id=1, source_target_pairs={{0,2},{1,3},{2,0},{3,1},{4,6},{5,7},{6,4},{7,5},{8,10},{9,11},{10,... | collective-permute-start | bytes 235016 | tf_op jit(solution)/shard_map/ppermute | solution.py:39
  118.5 7.0 %collective-permute-start.8 = (f32[128,153]{0,1:T(8,128)S(1)}, f32[128,153]{0,1:T(8,128)S(1)}, u32[]{:S(2)}, u32[]{:S(2)}) collective-permute-start(f32[128,153]{0,1:T(8,128)S(1)} %add_bitcast_fusion.2), channel_id=1, source_target_pairs={{0,4},{1,5},{2,6},{3,7},{4,0},{5,1},{6,2},{7,3},{8,12},{9,13},{10,... | collective-permute-start | bytes 235016 | tf_op jit(solution)/shard_map/ppermute | solution.py:39
  120.7 6.5 %collective-permute-start.9 = (f32[128,153]{0,1:T(8,128)S(1)}, f32[128,153]{0,1:T(8,128)S(1)}, u32[]{:S(2)}, u32[]{:S(2)}) collective-permute-start(f32[128,153]{0,1:T(8,128)S(1)} %add_bitcast_fusion.2), channel_id=1, source_target_pairs={{0,6},{1,7},{2,4},{3,5},{4,2},{5,3},{6,0},{7,1},{8,14},{9,15},{10,... | collective-permute-start | bytes 235016 | tf_op jit(solution)/shard_map/ppermute | solution.py:39
  127.3 6.4 %collective-permute-start.10 = (f32[128,153]{0,1:T(8,128)S(1)}, f32[128,153]{0,1:T(8,128)S(1)}, u32[]{:S(2)}, u32[]{:S(2)}) collective-permute-start(f32[128,153]{0,1:T(8,128)S(1)} %add_bitcast_fusion.1), channel_id=1, source_target_pairs={{0,32},{1,33},{2,34},{3,35},{4,36},{5,37},{6,38},{7,39},{8,40},{9,... | collective-permute-start | bytes 235016 | tf_op jit(solution)/shard_map/ppermute | solution.py:39
  130.0 5.9 %collective-permute-start.11 = (f32[128,153]{0,1:T(8,128)S(1)}, f32[128,153]{0,1:T(8,128)S(1)}, u32[]{:S(2)}, u32[]{:S(2)}) collective-permute-start(f32[128,153]{0,1:T(8,128)S(1)} %add_bitcast_fusion.1), channel_id=1, source_target_pairs={{0,64},{1,65},{2,66},{3,67},{4,68},{5,69},{6,70},{7,71},{8,72},{9,... | collective-permute-start | bytes 235016 | tf_op jit(solution)/shard_map/ppermute | solution.py:39
  131.8 6.0 %collective-permute-start.12 = (f32[128,153]{0,1:T(8,128)S(1)}, f32[128,153]{0,1:T(8,128)S(1)}, u32[]{:S(2)}, u32[]{:S(2)}) collective-permute-start(f32[128,153]{0,1:T(8,128)S(1)} %add_bitcast_fusion.1), channel_id=1, source_target_pairs={{0,96},{1,97},{2,98},{3,99},{4,100},{5,101},{6,102},{7,103},{8,104... | collective-permute-start | bytes 235016 | tf_op jit(solution)/shard_map/ppermute | solution.py:39
  137.8 4.9 %collective-permute-start.13 = (f32[128,153]{0,1:T(8,128)S(1)}, f32[128,153]{0,1:T(8,128)S(1)}, u32[]{:S(2)}, u32[]{:S(2)}) collective-permute-start(f32[128,153]{0,1:T(8,128)S(1)} %add_bitcast_fusion), channel_id=1, source_target_pairs={{0,1},{1,0},{2,3},{3,2},{4,5},{5,4},{6,7},{7,6},{8,9},{9,8},{10,11... | collective-permute-start | bytes 235016 | tf_op jit(solution)/shard_map/ppermute | solution.py:39
  (3 other events, 1.8 us)
where the time goes:
time: 145 us; the launch traced here: 144 us
  waiting for transfers between devices  52.7 us (36%)
  starting transfers between devices  35.9 us (25%)
  other arithmetic  30.1 us (21%)
  matrix products  14.5 us (10%)
  local copies, waits for them, and re-layouts  9.59 us (7%)
    ppermute x10, waiting for transfers between devices, group_sum(): lax.ppermute(value, MESH_AXES, [(d, d ^ mask) for d in range(count)])  19.1 us
    all_to_all x1, waiting for transfers between devices, layer(): arrived = lax.all_to_all(payload, 'lat', 0, 0, tiled=True)  18.1 us
    all_to_all x1, waiting for transfers between devices, layer(): own_rows = lax.all_to_all(by_device, MESH_AXES, 1, 0, tiled=True)  15.4 us
    ppermute x10, starting transfers between devices, group_sum(): lax.ppermute(value, MESH_AXES, [(d, d ^ mask) for d in range(count)])  12.3 us
    convert_element_type x1, other arithmetic, layer(): hidden = hidden.astype(jnp.bfloat16)  7.56 us
    all_to_all x1, starting transfers between devices, layer(): arrived = lax.all_to_all(payload, 'lat', 0, 0, tiled=True)  7.5 us
    ppermute x2, starting transfers between devices, with_rims(): upper = lax.ppermute(field[field.shape[0] - width:], MESH_AXES, down_pairs)  6.64 us
    add x4, other arithmetic, step(): grad_input + weight_tap * grad_pad[4 - tap_row:4 - tap_row + row_count, s...  6.25 us
  transfers between devices with their start and end apart: 16, of which 9 were waited for; matrix products, arithmetic and copies ran while one was open for 23% of the time, Pallas kernels for 0%

commit v1 on v0

--- a/solution.py
+++ b/solution.py
@@ -37,9 +37,15 @@
     for x in range(1, size):
         mask = mask_of(x)
         held.append(lax.ppermute(value, MESH_AXES, [(d, d ^ mask) for d in range(count)]))
-    held = jnp.stack(held)
     position = sum(((me >> bit) & 1) << i for i, bit in enumerate(bits))
-    members = [lax.dynamic_index_in_dim(held, position ^ j, keepdims=False) for j in range(size)]
+
+    def member(j):
+        chosen = held[size - 1]
+        for x in range(size - 2, -1, -1):
+            chosen = jnp.where((position ^ j) == x, held[x], chosen)
+        return chosen
+
+    members = [member(j) for j in range(size)]
     while len(members) > 1:
         members = [members[i] + members[i + 1] for i in range(0, len(members), 2)]
     return members[0]
@@ -127,12 +133,12 @@
     masked = masked.astype(grad_coef.dtype)
     arrived, hidden, masked = lax.optimization_barrier((arrived, hidden, masked))
     body = arrived[:, : own_slots * band_rows].reshape(n_lat, own_slots, band_rows, degrees)
-    leg_rows = body.transpose(1, 0, 2, 3).reshape(own_slots, n_lat * band_rows, degrees)
     parts = arrived[:, own_slots * band_rows, : 4 * band_rows].astype(jnp.float32)
     parts = parts.reshape(n_lat, 4, band_rows)
     weights = ((parts[:, 3] + parts[:, 2]) + parts[:, 1]) + parts[:, 0]
     weights = weights.reshape(-1)
-    summed = jnp.einsum("slj,sjk->slk", leg_rows, masked, preferred_element_type=jnp.float32)
+    summed = jnp.einsum("lsrj,sjk->slrk", body, masked, preferred_element_type=jnp.float32)
+    summed = summed.reshape(own_slots, n_lat * band_rows, doubled)
     spectral = (summed * weights[None, :, None]).astype(jnp.bfloat16)
     by_device = spectral.reshape(own_slots, n_lat, n_ord, row_count * doubled)
     by_device = by_device.transpose(0, 2, 1, 3).reshape(own_slots, n_ord * n_lat, -1)

time: 145 us -> 146 us (level)
  matrix products: 14.5 us -> 12.8 us
    dot_general x1, matrix products: 2.44 us -> 0.77 us  [layer(): jnp.einsum('lsrj,sjk->slrk', body, masked, preferred_element_type=jnp.flo...]
    unnamed x71 -> x73, local copies, waits for them, and re-layouts: 3.97 us -> 5.46 us
where the time goes in v1:
time: 146 us; the launch traced here: 145 us
  waiting for transfers between devices  52.7 us (36%)
  starting transfers between devices  35.9 us (25%)
  other arithmetic  31.1 us (21%)
  matrix products  12.8 us (9%)
  local copies, waits for them, and re-layouts  10.7 us (7%)
    ppermute x10, waiting for transfers between devices, group_sum(): lax.ppermute(value, MESH_AXES, [(d, d ^ mask) for d in range(count)])  19.1 us
    all_to_all x1, waiting for transfers between devices, layer(): arrived = lax.all_to_all(payload, 'lat', 0, 0, tiled=True)  18.2 us
    all_to_all x1, waiting for transfers between devices, layer(): own_rows = lax.all_to_all(by_device, MESH_AXES, 1, 0, tiled=True)  15.4 us
    ppermute x10, starting transfers between devices, group_sum(): lax.ppermute(value, MESH_AXES, [(d, d ^ mask) for d in range(count)])  12.3 us
    convert_element_type x1, other arithmetic, layer(): hidden = hidden.astype(jnp.bfloat16)  7.55 us
    all_to_all x1, starting transfers between devices, layer(): arrived = lax.all_to_all(payload, 'lat', 0, 0, tiled=True)  7.5 us
    ppermute x2, starting transfers between devices, with_rims(): upper = lax.ppermute(field[field.shape[0] - width:], MESH_AXES, down_pairs)  6.64 us
    add x4, other arithmetic, step(): grad_input + weight_tap * grad_pad[4 - tap_row:4 - tap_row + row_count, s...  6.25 us
  transfers between devices with their start and end apart: 16, of which 9 were waited for; matrix products, arithmetic and copies ran while one was open for 23% of the time, Pallas kernels for 0%

profile of v1, /device:TPU:1, one launch (start us, length us, event | category | flops | bytes accessed | tf_op | source)
XLA Modules:
  0.0 144.6 jit_solution(2482299444745766853)
XLA Ops:
  0.6 4.6 %collective-permute-start = (bf16[2,1440,128]{2,1,0:T(8,128)(2,1)}, bf16[2,1440,128]{2,1,0:T(8,128)(2,1)S(1)}, u32[]{:S(2)}, u32[]{:S(2)}) collective-permute-start(bf16[2,1440,128]{2,1,0:T(8,128)(2,1)} %bitcast.132), channel_id=1, source_target_pairs={{0,8},{8,16},{16,24},{24,32},{32,40},{40,48},{48,56},{56,64},{64,7... | collective-permute-start | bytes 2211848 | tf_op jit(solution)/shard_map/ppermute | solution.py:23
  5.2 1.9 %collective-permute-start.1 = (bf16[2,1440,128]{2,1,0:T(8,128)(2,1)}, bf16[2,1440,128]{2,1,0:T(8,128)(2,1)}, u32[]{:S(2)}, u32[]{:S(2)}) collective-permute-start(bf16[2,1440,128]{2,1,0:T(8,128)(2,1)} %bitcast.133), channel_id=1, source_target_pairs={{8,0},{16,8},{24,16},{32,24},{40,32},{48,40},{56,48},{64,56},{72,6... | collective-permute-start | bytes 2211848 | tf_op jit(solution)/shard_map/ppermute | solution.py:24
  7.9 3.3 %pad_maximum_fusion.1 = bf16[8,200,768]{2,1,0:T(8,128)(2,1)} fusion(bf16[8,8,768]{2,1,0:T(8,128)(2,1)S(1)} %broadcast_in_dim.8, bf16[8,192,768]{2,1,0:T(8,128)(2,1)} %bitcast.129), kind=kLoop, calls=%fused_computation.65 | loop fusion | flops 4915200 | bytes 4915200 | tf_op jit(solution)/shard_map/concatenate | solution.py:115
  11.2 7.5 %all-to-all-start = ((bf16[8,200,768]{2,1,0:T(8,128)(2,1)}), bf16[8,200,768]{2,1,0:T(8,128)(2,1)S(1)}, u32[]{:S(2)}, u32[]{:S(2)}) async-start(bf16[8,200,768]{2,1,0:T(8,128)(2,1)} %pad_maximum_fusion.1), calls=%async_computation | async-start | bytes 4915200 | tf_op jit(solution)/shard_map/all_to_all | solution.py:116
  20.1 1.3 fusion.140
  21.4 4.1 %fusion.5 = bf16[6,768,256]{2,1,0:T(8,128)(2,1)} fusion(bf16[6,768,256]{2,1,0:T(8,128)(2,1)} %param.8, bf16[6,768]{1,0:T(8,128)(2,1)S(1)} %fusion.144, s32[256]{0:T(256)S(1)} %fusion.157), kind=kOutput, calls=%fused_computation.109 | convolution fusion | flops 606404608 | bytes 4728832 | tf_op jit(solution)/shard_map/sjk,kt->sjt/dot_general | solution.py:132
  25.5 1.4 maximum_convert_fusion
  27.0 2.0 %copy-done.1 = f32[6,1440,128]{2,1,0:T(8,128)} copy-done((f32[6,1440,128]{2,1,0:T(8,128)}, f32[6,1440,128]{2,1,0:T(8,128)S(1)}, u32[]{:S(2)}) %copy-start.1) | copy-done | bytes 4423704
  29.0 7.5 %add_convert_fusion = (bf16[2,1440,128]{2,1,0:T(8,128)(2,1)}, f32[2,1440,128]{2,1,0:T(8,128)}, f32[2,1440,128]{2,1,0:T(8,128)}) fusion(f32[6,1440,128]{2,1,0:T(8,128)S(1)} %maximum_convert_fusion, f32[128]{0:T(128)S(1)} %get-tuple-element.98, f32[128]{0:T(128)S(1)} %get-tuple-element.99, f32[128]{0:T(128)S(1)} %get-tuple-element.76, ...), kind=kLoop, calls=%fused_computation.226 | loop fusion | flops 25804800 | bytes 15544832 | tf_op jit(solution)/shard_map/convert_element_type | solution.py:125
  36.6 18.2 %all-to-all-done = bf16[8,200,768]{2,1,0:T(8,128)(2,1)S(1)} async-done(((bf16[8,200,768]{2,1,0:T(8,128)(2,1)}), bf16[8,200,768]{2,1,0:T(8,128)(2,1)S(1)}, u32[]{:S(2)}, u32[]{:S(2)}) %all-to-all-start) | async-done | bytes 2457632 | tf_op jit(solution)/shard_map/all_to_all | solution.py:116
  54.9 1.5 %copy-done.33 = bf16[6,768,256]{2,1,0:T(8,128)(2,1)S(1)} copy-done((bf16[6,768,256]{2,1,0:T(8,128)(2,1)S(1)}, bf16[6,768,256]{2,1,0:T(8,128)(2,1)}, u32[]{:S(2)}) %copy-start.33) | copy-done | bytes 2359320
  56.4 0.8 fusion
  57.8 1.1 fusion.115
  59.0 1.5 %copy.26 = bf16[6,128,512]{2,0,1:T(8,128)(2,1)} copy(bf16[6,128,512]{2,1,0:T(8,128)(2,1)S(1)} %fusion.115) | data formatting | bytes 1572864 | tf_op jit(solution)/shard_map/reshape | solution.py:144
  60.4 5.1 %all-to-all-start.1 = ((bf16[6,128,512]{2,0,1:T(8,128)(2,1)}), bf16[6,128,512]{2,0,1:T(8,128)(2,1)S(1)}, u32[]{:S(2)}, u32[]{:S(2)}) async-start(bf16[6,128,512]{2,0,1:T(8,128)(2,1)} %copy.26), calls=%async_computation.1 | async-start | bytes 2097152 | tf_op jit(solution)/shard_map/all_to_all | solution.py:145
  65.5 1.6 %multiply_convert_fusion.1 = (bf16[1,36,40,768]{3,2,1,0:T(8,128)(2,1)S(1)}, bf16[1,36,40,768]{3,2,1,0:T(8,128)(2,1)S(1)}) fusion(f32[40,768]{1,0:T(8,128)S(1)} %get-tuple-element.105, f32[36,768]{1,0:T(8,128)S(1)} %copy-done.8, f32[40,768]{1,0:T(8,128)S(1)} %get-tuple-element.104, f32[36,768]{1,0:T(8,128)S(1)} %copy-done.7, f32[768]{0:T(1024)S(1)} %get-tuple-element.100, ...), kind=kLoop, calls=%fused_computation.63 | loop fusion | flops 11059200 | bytes 4896768 | tf_op jit(solution)/shard_map/convert.5
  67.1 2.5 %pad_maximum_fusion = bf16[2,36,40,768]{3,2,1,0:T(8,128)(2,1)} fusion(bf16[1,36,40,768]{3,2,1,0:T(8,128)(2,1)S(1)} %get-tuple-element.74, bf16[1,36,40,768]{3,2,1,0:T(8,128)(2,1)S(1)} %get-tuple-element.73), kind=kLoop, calls=%fused_computation.61 | loop fusion | flops 2211840 | bytes 8847360 | tf_op jit(solution)/shard_map/stack | solution.py:88
  69.6 15.4 %all-to-all-done.1 = bf16[6,128,512]{2,0,1:T(8,128)(2,1)S(1)} async-done(((bf16[6,128,512]{2,0,1:T(8,128)(2,1)}), bf16[6,128,512]{2,0,1:T(8,128)(2,1)S(1)}, u32[]{:S(2)}, u32[]{:S(2)}) %all-to-all-start.1) | async-done | bytes 786464 | tf_op jit(solution)/shard_map/all_to_all | solution.py:145
  85.4 1.1 fusion.165
  86.5 3.8 %fusion.118 = f32[2880,256]{1,0:T(8,128)S(1)} fusion(bf16[2880,768]{1,0:T(8,128)(2,1)} %bitcast.126, bf16[768,1,256]{2,1,0:T(2,128)(2,1)S(1)} %get-tuple-element.72), kind=kOutput, calls=%fused_computation.236 | convolution fusion | flops 1132462080 | bytes 7766016 | tf_op jit(solution)/shard_map/qs,sn->qn/dot_general | solution.py:152
  90.3 1.3 fusion.121
  91.8 2.5 %fusion.106 = (f32[128]{0:T(128)S(1)}, f32[128]{0:T(128)S(1)}, f32[128]{0:T(128)S(1)}, f32[128]{0:T(128)S(1)}, f32[128]{0:T(128)S(1)}, /*index=5*/f32[128]{0:T(1...) fusion(f32[6,1440,128]{2,1,0:T(8,128)S(1)} %bitcast.125, ...), kind=kOutput, calls=%fused_computation.209 | convolution fusion | flops 105429888 | bytes 5960192 | tf_op jit(solution)/shard_map/rqd,cd->rqc/dot_general | solution.py:156
  94.3 2.1 %collective-permute-start.5 = (bf16[2,1440,128]{2,1,0:T(8,128)(2,1)S(1)}, bf16[2,1440,128]{2,1,0:T(8,128)(2,1)S(1)}, u32[]{:S(2)}, u32[]{:S(2)}) collective-permute-start(bf16[2,1440,128]{2,1,0:T(8,128)(2,1)S(1)} %get-tuple-element.110), channel_id=1, source_target_pairs={{0,8},{8,16},{16,24},{24,32},{32,40},{40,48},{48,56},{56,64},{64,7... | collective-permute-start | bytes 2211848 | tf_op jit(solution)/shard_map/ppermute | solution.py:23
  96.4 2.4 %collective-permute-start.6 = (bf16[2,1440,128]{2,1,0:T(8,128)(2,1)S(1)}, bf16[2,1440,128]{2,1,0:T(8,128)(2,1)S(1)}, u32[]{:S(2)}, u32[]{:S(2)}) collective-permute-start(bf16[2,1440,128]{2,1,0:T(8,128)(2,1)S(1)} %get-tuple-element.110), channel_id=1, source_target_pairs={{8,0},{16,8},{24,16},{32,24},{40,32},{48,40},{56,48},{64,56},{72,6... | collective-permute-start | bytes 2211848 | tf_op jit(solution)/shard_map/ppermute | solution.py:24
  98.8 3.4 %fusion.109 = (f32[128]{0:T(128)S(1)}, f32[128]{0:T(128)S(1)}, f32[128]{0:T(128)S(1)}, f32[128]{0:T(128)S(1)}, f32[128]{0:T(128)S(1)}, /*index=5*/f32[128]{0:T(1...) fusion(bf16[2,1440,128]{2,1,0:T(8,128)(2,1)S(1)} %get-tuple-element.110, f32[6,8,128]{2,1,0:T(8,128)S(1)} %get-tuple-element.69, ...), kind=kLoop, calls=%fused_computation.212 | loop fusion | flops 10320768 | bytes 5190144 | tf_op jit(solution)/shard_map/reduce_sum | solution.py:166
  102.7 0.9 copy-done.3
  103.7 0.8 fusion.110
  104.6 1.3 collective-permute-start.3
  105.9 0.8 collective-permute-start.4
  106.7 8.6 %collective-permute-done.3 = f32[128,153]{0,1:T(8,128)S(1)} collective-permute-done((f32[128,153]{0,1:T(8,128)S(1)}, f32[128,153]{0,1:T(8,128)S(1)}, u32[]{:S(2)}, u32[]{:S(2)}) %collective-permute-start.3) | collective-permute-done | bytes 78368 | tf_op jit(solution)/shard_map/ppermute | solution.py:39
  115.3 0.9 collective-permute-done.4
  116.9 1.2 fusion.17
  118.1 0.8 collective-permute-start.7
  119.0 2.3 %collective-permute-start.8 = (f32[128,153]{0,1:T(8,128)S(1)}, f32[128,153]{0,1:T(8,128)S(1)}, u32[]{:S(2)}, u32[]{:S(2)}) collective-permute-start(f32[128,153]{0,1:T(8,128)S(1)} %add_add_fusion.2), channel_id=1, source_target_pairs={{0,4},{1,5},{2,6},{3,7},{4,0},{5,1},{6,2},{7,3},{8,12},{9,13},{10,... | collective-permute-start | bytes 235016 | tf_op jit(solution)/shard_map/ppermute | solution.py:39
  121.2 1.1 collective-permute-start.9
  122.3 1.3 fusion.25
  123.6 2.3 %collective-permute-done.8 = f32[128,153]{0,1:T(8,128)S(1)} collective-permute-done((f32[128,153]{0,1:T(8,128)S(1)}, f32[128,153]{0,1:T(8,128)S(1)}, u32[]{:S(2)}, u32[]{:S(2)}) %collective-permute-start.8) | collective-permute-done | bytes 78368 | tf_op jit(solution)/shard_map/ppermute | solution.py:39
  125.9 1.7 %collective-permute-done.9 = f32[128,153]{0,1:T(8,128)S(1)} collective-permute-done((f32[128,153]{0,1:T(8,128)S(1)}, f32[128,153]{0,1:T(8,128)S(1)}, u32[]{:S(2)}, u32[]{:S(2)}) %collective-permute-start.9) | collective-permute-done | bytes 78368 | tf_op jit(solution)/shard_map/ppermute | solution.py:39
  127.7 2.8 %collective-permute-start.10 = (f32[128,153]{0,1:T(8,128)S(1)}, f32[128,153]{0,1:T(8,128)S(1)}, u32[]{:S(2)}, u32[]{:S(2)}) collective-permute-start(f32[128,153]{0,1:T(8,128)S(1)} %add_add_fusion.1), channel_id=1, source_target_pairs={{0,32},{1,33},{2,34},{3,35},{4,36},{5,37},{6,38},{7,39},{8,40},{9,... | collective-permute-start | bytes 235016 | tf_op jit(solution)/shard_map/ppermute | solution.py:39
  130.5 1.8 %collective-permute-start.11 = (f32[128,153]{0,1:T(8,128)S(1)}, f32[128,153]{0,1:T(8,128)S(1)}, u32[]{:S(2)}, u32[]{:S(2)}) collective-permute-start(f32[128,153]{0,1:T(8,128)S(1)} %add_add_fusion.1), channel_id=1, source_target_pairs={{0,64},{1,65},{2,66},{3,67},{4,68},{5,69},{6,70},{7,71},{8,72},{9,... | collective-permute-start | bytes 235016 | tf_op jit(solution)/shard_map/ppermute | solution.py:39
  132.3 0.7 collective-permute-start.12
  133.0 1.1 fusion.34
  134.2 2.3 %collective-permute-done.11 = f32[128,153]{0,1:T(8,128)S(1)} collective-permute-done((f32[128,153]{0,1:T(8,128)S(1)}, f32[128,153]{0,1:T(8,128)S(1)}, u32[]{:S(2)}, u32[]{:S(2)}) %collective-permute-start.11) | collective-permute-done | bytes 78368 | tf_op jit(solution)/shard_map/ppermute | solution.py:39
  136.5 1.8 %collective-permute-done.12 = f32[128,153]{0,1:T(8,128)S(1)} collective-permute-done((f32[128,153]{0,1:T(8,128)S(1)}, f32[128,153]{0,1:T(8,128)S(1)}, u32[]{:S(2)}, u32[]{:S(2)}) %collective-permute-start.12) | collective-permute-done | bytes 78368 | tf_op jit(solution)/shard_map/ppermute | solution.py:39
  138.3 0.7 collective-permute-start.13
  139.0 2.6 %fusion.12 = bf16[2,1440,128]{2,1,0:T(8,128)(2,1)} fusion(f32[6,1440,128]{2,1,0:T(8,128)S(1)} %maximum_convert_fusion.1, f32[2,1440,128]{2,1,0:T(8,128)S(1)} %fusion.34, f32[6,8,128]{2,1,0:T(8,128)S(1)} %get-tuple-element.68, f32[6,8,128]{2,1,0:T(8,128)S(1)} %get-tuple-element.67, f32[128]{0:T(128)S(1)} %get-tuple-element.98, f32[128]{0:T(128)S(1)} %get-tuple-element.99, ...), kind=kLoop, calls=%fused_computation.115 | loop fusion | flops 7741440 | bytes 8162816 | tf_op jit(solution)/shard_map/add | solution.py:178
  141.6 1.6 %collective-permute-done.13 = f32[128,153]{0,1:T(8,128)S(1)} collective-permute-done((f32[128,153]{0,1:T(8,128)S(1)}, f32[128,153]{0,1:T(8,128)S(1)}, u32[]{:S(2)}, u32[]{:S(2)}) %collective-permute-start.13) | collective-permute-done | bytes 78368 | tf_op jit(solution)/shard_map/ppermute | solution.py:39
  143.8 0.7 copy.27
  (109 shorter events, 5.6 us)
Async XLA Ops:
  0.6 91.2 %copy-start = (bf16[128,128]{1,0:T(8,128)(2,1)S(1)}, bf16[128,128]{1,0:T(8,128)(2,1)}, u32[]{:S(2)}) copy-start(bf16[128,128]{1,0:T(8,128)(2,1)} %param.15) | copy-start | bytes 98308
  0.6 24.8 %collective-permute-start = (bf16[2,1440,128]{2,1,0:T(8,128)(2,1)}, bf16[2,1440,128]{2,1,0:T(8,128)(2,1)S(1)}, u32[]{:S(2)}, u32[]{:S(2)}) collective-permute-start(bf16[2,1440,128]{2,1,0:T(8,128)(2,1)} %bitcast.132), channel_id=1, source_target_pairs={{0,8},{8,16},{16,24},{24,32},{32,40},{40,48},{48,56},{56,64},{64,7... | collective-permute-start | bytes 2211848 | tf_op jit(solution)/shard_map/ppermute | solution.py:23
  5.2 20.3 %collective-permute-start.1 = (bf16[2,1440,128]{2,1,0:T(8,128)(2,1)}, bf16[2,1440,128]{2,1,0:T(8,128)(2,1)}, u32[]{:S(2)}, u32[]{:S(2)}) collective-permute-start(bf16[2,1440,128]{2,1,0:T(8,128)(2,1)} %bitcast.133), channel_id=1, source_target_pairs={{8,0},{16,8},{24,16},{32,24},{40,32},{48,40},{56,48},{64,56},{72,6... | collective-permute-start | bytes 2211848 | tf_op jit(solution)/shard_map/ppermute | solution.py:24
  11.2 7.5 %copy-start.9 = (s32[768]{0:T(1024)S(1)}, s32[768]{0:T(1024)}, u32[]{:S(2)}) copy-start(s32[768]{0:T(1024)} %param.11) | copy-start | bytes 9220
  11.2 8.1 %copy-start.10 = (f32[128,25]{0,1:T(8,128)S(1)}, f32[128,25]{0,1:T(8,128)}, u32[]{:S(2)}) copy-start(f32[128,25]{0,1:T(8,128)} %param.14) | copy-start | bytes 38404
  11.2 8.7 %copy-start.32 = (s32[48]{0:T(128)S(1)}, s32[48]{0:T(128)}, u32[]{:S(2)}) copy-start(s32[48]{0:T(128)} %param.12) | copy-start | bytes 580
  11.2 43.5 %all-to-all-start = ((bf16[8,200,768]{2,1,0:T(8,128)(2,1)}), bf16[8,200,768]{2,1,0:T(8,128)(2,1)S(1)}, u32[]{:S(2)}, u32[]{:S(2)}) async-start(bf16[8,200,768]{2,1,0:T(8,128)(2,1)} %pad_maximum_fusion.1), calls=%async_computation | async-start | bytes 4915200 | tf_op jit(solution)/shard_map/all_to_all | solution.py:116
  20.1 6.9 %copy-start.12 = (f32[128]{0:T(128)}, f32[128]{0:T(128)S(1)}, u32[]{:S(2)}) copy-start(f32[128]{0:T(128)S(1)} %get-tuple-element.94) | copy-start | bytes 1540
  20.1 6.9 %copy-start.14 = (f32[128]{0:T(128)}, f32[128]{0:T(128)S(1)}, u32[]{:S(2)}) copy-start(f32[128]{0:T(128)S(1)} %get-tuple-element.95) | copy-start | bytes 1540
  20.1 6.9 %copy-start.16 = (f32[128]{0:T(128)}, f32[128]{0:T(128)S(1)}, u32[]{:S(2)}) copy-start(f32[128]{0:T(128)S(1)} %get-tuple-element.96) | copy-start | bytes 1540
  20.1 6.9 %copy-start.18 = (f32[128]{0:T(128)}, f32[128]{0:T(128)S(1)}, u32[]{:S(2)}) copy-start(f32[128]{0:T(128)S(1)} %get-tuple-element.97) | copy-start | bytes 1540
  21.4 4.1 %copy-start.6 = (bf16[2,128,1440]{1,2,0:T(8,128)(2,1)S(1)}, bf16[2,128,1440]{1,2,0:T(8,128)(2,1)}, u32[]{:S(2)}) copy-start(bf16[2,128,1440]{1,2,0:T(8,128)(2,1)} %param.13) | copy-start | bytes 2211844
  25.4 3.5 %copy-start.11 = (f32[128]{0:T(128)S(1)}, f32[128]{0:T(128)}, u32[]{:S(2)}) copy-start(f32[128]{0:T(128)} %get-tuple-element.93) | copy-start | bytes 1540
  25.4 3.5 %copy-start.20 = (f32[128]{0:T(128)S(1)}, f32[128]{0:T(128)}, u32[]{:S(2)}) copy-start(f32[128]{0:T(128)} %get-tuple-element.87) | copy-start | bytes 1540
  25.4 3.5 %copy-start.22 = (f32[128]{0:T(128)S(1)}, f32[128]{0:T(128)}, u32[]{:S(2)}) copy-start(f32[128]{0:T(128)} %get-tuple-element.88) | copy-start | bytes 1540
  25.4 3.5 %copy-start.24 = (f32[128]{0:T(128)S(1)}, f32[128]{0:T(128)}, u32[]{:S(2)}) copy-start(f32[128]{0:T(128)} %get-tuple-element.89) | copy-start | bytes 1540
  25.5 3.5 %copy-start.26 = (f32[128]{0:T(128)S(1)}, f32[128]{0:T(128)}, u32[]{:S(2)}) copy-start(f32[128]{0:T(128)} %get-tuple-element.90) | copy-start | bytes 1540
  25.5 3.5 %copy-start.28 = (f32[128]{0:T(128)S(1)}, f32[128]{0:T(128)}, u32[]{:S(2)}) copy-start(f32[128]{0:T(128)} %get-tuple-element.91) | copy-start | bytes 1540
  25.5 3.5 %copy-start.30 = (f32[128]{0:T(128)S(1)}, f32[128]{0:T(128)}, u32[]{:S(2)}) copy-start(f32[128]{0:T(128)} %get-tuple-element.92) | copy-start | bytes 1540
  27.0 2.0 %copy-start.1 = (f32[6,1440,128]{2,1,0:T(8,128)}, f32[6,1440,128]{2,1,0:T(8,128)S(1)}, u32[]{:S(2)}) copy-start(f32[6,1440,128]{2,1,0:T(8,128)S(1)} %maximum_convert_fusion) | copy-start | bytes 13271044
  54.7 1.7 %copy-start.33 = (bf16[6,768,256]{2,1,0:T(8,128)(2,1)S(1)}, bf16[6,768,256]{2,1,0:T(8,128)(2,1)}, u32[]{:S(2)}) copy-start(bf16[6,768,256]{2,1,0:T(8,128)(2,1)} %fusion.5) | copy-start | bytes 7077892
  60.4 5.1 %copy-start.7 = (f32[36,768]{1,0:T(8,128)S(1)}, f32[36,768]{1,0:T(8,128)}, u32[]{:S(2)}) copy-start(f32[36,768]{1,0:T(8,128)} %get-tuple-element.102) | copy-start | bytes 331780
  60.4 5.1 %copy-start.8 = (f32[36,768]{1,0:T(8,128)S(1)}, f32[36,768]{1,0:T(8,128)}, u32[]{:S(2)}) copy-start(f32[36,768]{1,0:T(8,128)} %get-tuple-element.103) | copy-start | bytes 331780
  60.4 24.5 %all-to-all-start.1 = ((bf16[6,128,512]{2,0,1:T(8,128)(2,1)}), bf16[6,128,512]{2,0,1:T(8,128)(2,1)S(1)}, u32[]{:S(2)}, u32[]{:S(2)}) async-start(bf16[6,128,512]{2,0,1:T(8,128)(2,1)} %copy.26), calls=%async_computation.1 | async-start | bytes 2097152 | tf_op jit(solution)/shard_map/all_to_all | solution.py:145
  86.5 3.8 %copy-start.2 = (bf16[2,36,40,768]{3,2,1,0:T(8,128)(2,1)S(1)}, bf16[2,36,40,768]{3,2,1,0:T(8,128)(2,1)}, u32[]{:S(2)}) copy-start(bf16[2,36,40,768]{3,2,1,0:T(8,128)(2,1)} %pad_maximum_fusion) | copy-start | bytes 13271044
  86.5 5.3 %slice-start = ((s8[4423680]{0:T(1024)(128)(4,1)}), s8[4194304]{0:T(1024)(128)(4,1)S(1)}, s32[]{:S(2)}) async-start(s8[4423680]{0:T(1024)(128)(4,1)} %bitcast.124), calls=%async_computation.2 | async-start | bytes 8388608
  90.3 1.5 %slice-start.1 = ((s8[4423680]{0:T(1024)(128)(4,1)}), s8[229376]{0:T(1024)(128)(4,1)S(1)}, s32[]{:S(2)}) async-start(s8[4423680]{0:T(1024)(128)(4,1)} %bitcast.124), calls=%async_computation.3 | async-start | bytes 458752
  94.3 8.0 %copy-start.5 = (bf16[2,1440,128]{2,1,0:T(8,128)(2,1)S(1)}, bf16[2,1440,128]{2,1,0:T(8,128)(2,1)}, u32[]{:S(2)}) copy-start(bf16[2,1440,128]{2,1,0:T(8,128)(2,1)} %get-tuple-element.14) | copy-start | bytes 2211844
  94.3 21.9 %collective-permute-start.5 = (bf16[2,1440,128]{2,1,0:T(8,128)(2,1)S(1)}, bf16[2,1440,128]{2,1,0:T(8,128)(2,1)S(1)}, u32[]{:S(2)}, u32[]{:S(2)}) collective-permute-start(bf16[2,1440,128]{2,1,0:T(8,128)(2,1)S(1)} %get-tuple-element.110), channel_id=1, source_target_pairs={{0,8},{8,16},{16,24},{24,32},{32,40},{40,48},{48,56},{56,64},{64,7... | collective-permute-start | bytes 2211848 | tf_op jit(solution)/shard_map/ppermute | solution.py:23
  96.4 19.9 %collective-permute-start.6 = (bf16[2,1440,128]{2,1,0:T(8,128)(2,1)S(1)}, bf16[2,1440,128]{2,1,0:T(8,128)(2,1)S(1)}, u32[]{:S(2)}, u32[]{:S(2)}) collective-permute-start(bf16[2,1440,128]{2,1,0:T(8,128)(2,1)S(1)} %get-tuple-element.110), channel_id=1, source_target_pairs={{8,0},{16,8},{24,16},{32,24},{40,32},{48,40},{56,48},{64,56},{72,6... | collective-permute-start | bytes 2211848 | tf_op jit(solution)/shard_map/ppermute | solution.py:24
  98.8 3.9 %copy-start.4 = (f32[2,1440,128]{2,1,0:T(8,128)S(1)}, f32[2,1440,128]{2,1,0:T(8,128)}, u32[]{:S(2)}) copy-start(f32[2,1440,128]{2,1,0:T(8,128)} %get-tuple-element.66) | copy-start | bytes 4423684
  102.3 1.4 copy-start.3
  104.5 2.2 %collective-permute-start.2 = (f32[128,153]{0,1:T(8,128)S(1)}, f32[128,153]{0,1:T(8,128)S(1)}, u32[]{:S(2)}, u32[]{:S(2)}) collective-permute-start(f32[128,153]{0,1:T(8,128)S(1)} %concatenate.70), channel_id=1, source_target_pairs={{0,8},{1,9},{2,10},{3,11},{4,12},{5,13},{6,14},{7,15},{8,0},{9,1},... | collective-permute-start | bytes 235016 | tf_op jit(solution)/shard_map/ppermute | solution.py:39
  104.6 10.7 %collective-permute-start.3 = (f32[128,153]{0,1:T(8,128)S(1)}, f32[128,153]{0,1:T(8,128)S(1)}, u32[]{:S(2)}, u32[]{:S(2)}) collective-permute-start(f32[128,153]{0,1:T(8,128)S(1)} %concatenate.70), channel_id=1, source_target_pairs={{0,16},{1,17},{2,18},{3,19},{4,20},{5,21},{6,22},{7,23},{8,24},{9,... | collective-permute-start | bytes 235016 | tf_op jit(solution)/shard_map/ppermute | solution.py:39
  105.9 10.3 %collective-permute-start.4 = (f32[128,153]{0,1:T(8,128)S(1)}, f32[128,153]{0,1:T(8,128)S(1)}, u32[]{:S(2)}, u32[]{:S(2)}) collective-permute-start(f32[128,153]{0,1:T(8,128)S(1)} %concatenate.70), channel_id=1, source_target_pairs={{0,24},{1,25},{2,26},{3,27},{4,28},{5,29},{6,30},{7,31},{8,16},{9,... | collective-permute-start | bytes 235016 | tf_op jit(solution)/shard_map/ppermute | solution.py:39
  116.9 5.4 %copy-start.21 = (f32[128]{0:T(128)S(1)}, f32[128]{0:T(128)}, u32[]{:S(2)}) copy-start(f32[128]{0:T(128)} %get-tuple-element.87) | copy-start | bytes 1540
  116.9 5.4 %copy-start.23 = (f32[128]{0:T(128)S(1)}, f32[128]{0:T(128)}, u32[]{:S(2)}) copy-start(f32[128]{0:T(128)} %get-tuple-element.88) | copy-start | bytes 1540
  116.9 5.4 %copy-start.25 = (f32[128]{0:T(128)S(1)}, f32[128]{0:T(128)}, u32[]{:S(2)}) copy-start(f32[128]{0:T(128)} %get-tuple-element.89) | copy-start | bytes 1540
  116.9 5.4 %copy-start.27 = (f32[128]{0:T(128)S(1)}, f32[128]{0:T(128)}, u32[]{:S(2)}) copy-start(f32[128]{0:T(128)} %get-tuple-element.90) | copy-start | bytes 1540
  116.9 5.4 %copy-start.29 = (f32[128]{0:T(128)S(1)}, f32[128]{0:T(128)}, u32[]{:S(2)}) copy-start(f32[128]{0:T(128)} %get-tuple-element.91) | copy-start | bytes 1540
  116.9 5.4 %copy-start.31 = (f32[128]{0:T(128)S(1)}, f32[128]{0:T(128)}, u32[]{:S(2)}) copy-start(f32[128]{0:T(128)} %get-tuple-element.92) | copy-start | bytes 1540
  118.1 5.5 %collective-permute-start.7 = (f32[128,153]{0,1:T(8,128)S(1)}, f32[128,153]{0,1:T(8,128)S(1)}, u32[]{:S(2)}, u32[]{:S(2)}) collective-permute-start(f32[128,153]{0,1:T(8,128)S(1)} %add_add_fusion.2), channel_id=1, source_target_pairs={{0,2},{1,3},{2,0},{3,1},{4,6},{5,7},{6,4},{7,5},{8,10},{9,11},{10,... | collective-permute-start | bytes 235016 | tf_op jit(solution)/shard_map/ppermute | solution.py:39
  119.0 7.0 %collective-permute-start.8 = (f32[128,153]{0,1:T(8,128)S(1)}, f32[128,153]{0,1:T(8,128)S(1)}, u32[]{:S(2)}, u32[]{:S(2)}) collective-permute-start(f32[128,153]{0,1:T(8,128)S(1)} %add_add_fusion.2), channel_id=1, source_target_pairs={{0,4},{1,5},{2,6},{3,7},{4,0},{5,1},{6,2},{7,3},{8,12},{9,13},{10,... | collective-permute-start | bytes 235016 | tf_op jit(solution)/shard_map/ppermute | solution.py:39
  121.2 6.5 %collective-permute-start.9 = (f32[128,153]{0,1:T(8,128)S(1)}, f32[128,153]{0,1:T(8,128)S(1)}, u32[]{:S(2)}, u32[]{:S(2)}) collective-permute-start(f32[128,153]{0,1:T(8,128)S(1)} %add_add_fusion.2), channel_id=1, source_target_pairs={{0,6},{1,7},{2,4},{3,5},{4,2},{5,3},{6,0},{7,1},{8,14},{9,15},{10,... | collective-permute-start | bytes 235016 | tf_op jit(solution)/shard_map/ppermute | solution.py:39
  127.7 6.4 %collective-permute-start.10 = (f32[128,153]{0,1:T(8,128)S(1)}, f32[128,153]{0,1:T(8,128)S(1)}, u32[]{:S(2)}, u32[]{:S(2)}) collective-permute-start(f32[128,153]{0,1:T(8,128)S(1)} %add_add_fusion.1), channel_id=1, source_target_pairs={{0,32},{1,33},{2,34},{3,35},{4,36},{5,37},{6,38},{7,39},{8,40},{9,... | collective-permute-start | bytes 235016 | tf_op jit(solution)/shard_map/ppermute | solution.py:39
  130.5 5.9 %collective-permute-start.11 = (f32[128,153]{0,1:T(8,128)S(1)}, f32[128,153]{0,1:T(8,128)S(1)}, u32[]{:S(2)}, u32[]{:S(2)}) collective-permute-start(f32[128,153]{0,1:T(8,128)S(1)} %add_add_fusion.1), channel_id=1, source_target_pairs={{0,64},{1,65},{2,66},{3,67},{4,68},{5,69},{6,70},{7,71},{8,72},{9,... | collective-permute-start | bytes 235016 | tf_op jit(solution)/shard_map/ppermute | solution.py:39
  132.3 6.0 %collective-permute-start.12 = (f32[128,153]{0,1:T(8,128)S(1)}, f32[128,153]{0,1:T(8,128)S(1)}, u32[]{:S(2)}, u32[]{:S(2)}) collective-permute-start(f32[128,153]{0,1:T(8,128)S(1)} %add_add_fusion.1), channel_id=1, source_target_pairs={{0,96},{1,97},{2,98},{3,99},{4,100},{5,101},{6,102},{7,103},{8,104... | collective-permute-start | bytes 235016 | tf_op jit(solution)/shard_map/ppermute | solution.py:39
  138.3 4.9 %collective-permute-start.13 = (f32[128,153]{0,1:T(8,128)S(1)}, f32[128,153]{0,1:T(8,128)S(1)}, u32[]{:S(2)}, u32[]{:S(2)}) collective-permute-start(f32[128,153]{0,1:T(8,128)S(1)} %add_add_fusion), channel_id=1, source_target_pairs={{0,1},{1,0},{2,3},{3,2},{4,5},{5,4},{6,7},{7,6},{8,9},{9,8},{10,11... | collective-permute-start | bytes 235016 | tf_op jit(solution)/shard_map/ppermute | solution.py:39
  (4 other events, 2.4 us)

commit v2 on v1

--- a/solution.py
+++ b/solution.py
@@ -133,12 +133,12 @@
     masked = masked.astype(grad_coef.dtype)
     arrived, hidden, masked = lax.optimization_barrier((arrived, hidden, masked))
     body = arrived[:, : own_slots * band_rows].reshape(n_lat, own_slots, band_rows, degrees)
+    leg_rows = body.transpose(1, 0, 2, 3).reshape(own_slots, n_lat * band_rows, degrees)
     parts = arrived[:, own_slots * band_rows, : 4 * band_rows].astype(jnp.float32)
     parts = parts.reshape(n_lat, 4, band_rows)
     weights = ((parts[:, 3] + parts[:, 2]) + parts[:, 1]) + parts[:, 0]
     weights = weights.reshape(-1)
-    summed = jnp.einsum("lsrj,sjk->slrk", body, masked, preferred_element_type=jnp.float32)
-    summed = summed.reshape(own_slots, n_lat * band_rows, doubled)
+    summed = jnp.einsum("slj,sjk->slk", leg_rows, masked, preferred_element_type=jnp.float32)
     spectral = (summed * weights[None, :, None]).astype(jnp.bfloat16)
     by_device = spectral.reshape(own_slots, n_lat, n_ord, row_count * doubled)
     by_device = by_device.transpose(0, 2, 1, 3).reshape(own_slots, n_ord * n_lat, -1)
@@ -167,7 +167,7 @@
     depth_part = jnp.stack(depth_terms, axis=1)
     grad_pad = wrap_longitudes(with_rims(grad_hidden).astype(jnp.float32), WRAP)
     taps = [(tap_row, tap_col) for tap_row in range(5) for tap_col in range(5)]
-    rounds = 4
+    rounds = 3
     groups = [taps[i * len(taps) // rounds : (i + 1) * len(taps) // rounds] for i in range(rounds)]
 
     def tap_group(group):
@@ -182,13 +182,15 @@
 
         return step
 
+    def finish(grad_input):
+        return grad_input.astype(jnp.bfloat16).transpose(0, 2, 1)
+
     grad_input = jnp.zeros((row_count, longitudes, channels), jnp.float32)
     sums, grad_input = butterfly_sum(
         jnp.concatenate([point_part, depth_part], axis=1),
         grad_input,
-        [tap_group(group) for group in groups],
+        [tap_group(group) for group in groups] + [finish],
     )
-    grad_input = grad_input.astype(jnp.bfloat16).transpose(0, 2, 1)
     total_rows = row_count * n_ord * n_lat
     grad_scale = 1.0 / math.sqrt(total_rows * longitudes)
     sums = sums * grad_scale

time: 146 us -> 146 us (level)
  matrix products: 12.8 us -> 14.5 us
    dot_general x1, matrix products: 0.77 us -> 2.44 us  [layer(): jnp.einsum('slj,sjk->slk', leg_rows, masked, preferred_element_type=jnp.f...]
    unnamed x73 -> x63, local copies, waits for them, and re-layouts: 5.46 us -> 3.97 us
    add x4 -> x3, other arithmetic: 6.25 us -> 6.09 us  [step(): grad_input + weight_tap * grad_pad[4 - tap_row:4 - tap_row + row_count, s...]
where the time goes in v2:
time: 146 us; the launch traced here: 145 us
  waiting for transfers between devices  53.3 us (37%)
  starting transfers between devices  35.7 us (24%)
  other arithmetic  29.9 us (20%)
  matrix products  14.5 us (10%)
  local copies, waits for them, and re-layouts  10.1 us (7%)
    ppermute x10, waiting for transfers between devices, group_sum(): lax.ppermute(value, MESH_AXES, [(d, d ^ mask) for d in range(count)])  19.7 us
    all_to_all x1, waiting for transfers between devices, layer(): arrived = lax.all_to_all(payload, 'lat', 0, 0, tiled=True)  18.2 us
    all_to_all x1, waiting for transfers between devices, layer(): own_rows = lax.all_to_all(by_device, MESH_AXES, 1, 0, tiled=True)  15.4 us
    ppermute x10, starting transfers between devices, group_sum(): lax.ppermute(value, MESH_AXES, [(d, d ^ mask) for d in range(count)])  12.1 us
    convert_element_type x1, other arithmetic, layer(): hidden = hidden.astype(jnp.bfloat16)  7.52 us
    all_to_all x1, starting transfers between devices, layer(): arrived = lax.all_to_all(payload, 'lat', 0, 0, tiled=True)  7.5 us
    ppermute x2, starting transfers between devices, with_rims(): upper = lax.ppermute(field[field.shape[0] - width:], MESH_AXES, down_pairs)  6.64 us
    add x3, other arithmetic, step(): grad_input + weight_tap * grad_pad[4 - tap_row:4 - tap_row + row_count, s...  6.09 us
  transfers between devices with their start and end apart: 16, of which 9 were waited for; matrix products, arithmetic and copies ran while one was open for 23% of the time, Pallas kernels for 0%

profile of v2, /device:TPU:1, one launch (start us, length us, event | category | flops | bytes accessed | tf_op | source)
XLA Modules:
  0.0 144.7 jit_solution(10168565271315212930)
XLA Ops:
  0.6 4.6 %collective-permute-start = (bf16[2,1440,128]{2,1,0:T(8,128)(2,1)}, bf16[2,1440,128]{2,1,0:T(8,128)(2,1)S(1)}, u32[]{:S(2)}, u32[]{:S(2)}) collective-permute-start(bf16[2,1440,128]{2,1,0:T(8,128)(2,1)} %bitcast.129), channel_id=1, source_target_pairs={{0,8},{8,16},{16,24},{24,32},{32,40},{40,48},{48,56},{56,64},{64,7... | collective-permute-start | bytes 2211848 | tf_op jit(solution)/shard_map/ppermute | solution.py:23
  5.2 1.9 %collective-permute-start.1 = (bf16[2,1440,128]{2,1,0:T(8,128)(2,1)}, bf16[2,1440,128]{2,1,0:T(8,128)(2,1)}, u32[]{:S(2)}, u32[]{:S(2)}) collective-permute-start(bf16[2,1440,128]{2,1,0:T(8,128)(2,1)} %bitcast.130), channel_id=1, source_target_pairs={{8,0},{16,8},{24,16},{32,24},{40,32},{48,40},{56,48},{64,56},{72,6... | collective-permute-start | bytes 2211848 | tf_op jit(solution)/shard_map/ppermute | solution.py:24
  7.2 0.7 reduce-precision_convert_fusion.2
  7.9 3.3 %pad_maximum_fusion.1 = bf16[8,200,768]{2,1,0:T(8,128)(2,1)} fusion(bf16[8,8,768]{2,1,0:T(8,128)(2,1)S(1)} %broadcast_in_dim.8, bf16[8,192,768]{2,1,0:T(8,128)(2,1)} %bitcast.127), kind=kLoop, calls=%fused_computation.65 | loop fusion | flops 4915200 | bytes 4915200 | tf_op jit(solution)/shard_map/concatenate | solution.py:115
  11.2 7.5 %all-to-all-start = ((bf16[8,200,768]{2,1,0:T(8,128)(2,1)}), bf16[8,200,768]{2,1,0:T(8,128)(2,1)S(1)}, u32[]{:S(2)}, u32[]{:S(2)}) async-start(bf16[8,200,768]{2,1,0:T(8,128)(2,1)} %pad_maximum_fusion.1), calls=%async_computation | async-start | bytes 4915200 | tf_op jit(solution)/shard_map/all_to_all | solution.py:116
  19.3 0.6 slice_bitcast_fusion.24
  20.1 1.3 fusion.135
  21.4 4.1 %fusion.2 = bf16[6,768,256]{2,1,0:T(8,128)(2,1)} fusion(bf16[6,768,256]{2,1,0:T(8,128)(2,1)} %param.8, bf16[6,768]{1,0:T(8,128)(2,1)S(1)} %fusion.139, s32[256]{0:T(256)S(1)} %fusion.153), kind=kOutput, calls=%fused_computation.106 | convolution fusion | flops 606404608 | bytes 4728832 | tf_op jit(solution)/shard_map/sjk,kt->sjt/dot_general | solution.py:132
  25.5 1.4 maximum_convert_fusion
  27.0 2.0 %copy-done.1 = f32[6,1440,128]{2,1,0:T(8,128)} copy-done((f32[6,1440,128]{2,1,0:T(8,128)}, f32[6,1440,128]{2,1,0:T(8,128)S(1)}, u32[]{:S(2)}) %copy-start.1) | copy-done | bytes 4423704
  29.0 7.5 %add_convert_fusion = (bf16[2,1440,128]{2,1,0:T(8,128)(2,1)}, f32[2,1440,128]{2,1,0:T(8,128)}, f32[2,1440,128]{2,1,0:T(8,128)}) fusion(f32[6,1440,128]{2,1,0:T(8,128)S(1)} %maximum_convert_fusion, f32[128]{0:T(128)S(1)} %get-tuple-element.98, f32[128]{0:T(128)S(1)} %get-tuple-element.99, f32[128]{0:T(128)S(1)} %get-tuple-element.76, ...), kind=kLoop, calls=%fused_computation.222 | loop fusion | flops 25804800 | bytes 15544832 | tf_op jit(solution)/shard_map/convert_element_type | solution.py:125
  36.5 18.2 %all-to-all-done = bf16[8,200,768]{2,1,0:T(8,128)(2,1)S(1)} async-done(((bf16[8,200,768]{2,1,0:T(8,128)(2,1)}), bf16[8,200,768]{2,1,0:T(8,128)(2,1)S(1)}, u32[]{:S(2)}, u32[]{:S(2)}) %all-to-all-start) | async-done | bytes 2457632 | tf_op jit(solution)/shard_map/all_to_all | solution.py:116
  55.2 0.6 add.323
  55.9 2.4 %multiply_convert_fusion.2 = bf16[6,256,256]{2,1,0:T(8,128)(2,1)S(1)} fusion(bf16[6,256,768]{2,1,0:T(8,128)(2,1)S(1)} %bitcast.128, bf16[6,768,256]{2,1,0:T(8,128)(2,1)} %fusion.2, f32[256]{0:T(256)} %add.323), kind=kOutput, calls=%fused_computation.107 | convolution fusion | flops 604766208 | bytes 5506048 | tf_op jit(solution)/shard_map/slj,sjk->slk/dot_general | solution.py:141
  59.0 1.5 %copy.18 = bf16[6,128,512]{2,0,1:T(8,128)(2,1)} copy(bf16[6,128,512]{2,1,0:T(8,128)(2,1)S(1)} %bitcast.126) | data formatting | bytes 1572864 | tf_op jit(solution)/shard_map/reshape | solution.py:144
  60.5 5.1 %all-to-all-start.1 = ((bf16[6,128,512]{2,0,1:T(8,128)(2,1)}), bf16[6,128,512]{2,0,1:T(8,128)(2,1)S(1)}, u32[]{:S(2)}, u32[]{:S(2)}) async-start(bf16[6,128,512]{2,0,1:T(8,128)(2,1)} %copy.18), calls=%async_computation.1 | async-start | bytes 2097152 | tf_op jit(solution)/shard_map/all_to_all | solution.py:145
  65.6 1.6 %multiply_convert_fusion.1 = (bf16[1,36,40,768]{3,2,1,0:T(8,128)(2,1)S(1)}, bf16[1,36,40,768]{3,2,1,0:T(8,128)(2,1)S(1)}) fusion(f32[40,768]{1,0:T(8,128)S(1)} %get-tuple-element.105, f32[36,768]{1,0:T(8,128)S(1)} %copy-done.8, f32[40,768]{1,0:T(8,128)S(1)} %get-tuple-element.104, f32[36,768]{1,0:T(8,128)S(1)} %copy-done.7, f32[768]{0:T(1024)S(1)} %get-tuple-element.100, ...), kind=kLoop, calls=%fused_computation.63 | loop fusion | flops 11059200 | bytes 4896768 | tf_op jit(solution)/shard_map/convert.5
  67.1 2.5 %pad_maximum_fusion = bf16[2,36,40,768]{3,2,1,0:T(8,128)(2,1)} fusion(bf16[1,36,40,768]{3,2,1,0:T(8,128)(2,1)S(1)} %get-tuple-element.74, bf16[1,36,40,768]{3,2,1,0:T(8,128)(2,1)S(1)} %get-tuple-element.73), kind=kLoop, calls=%fused_computation.61 | loop fusion | flops 2211840 | bytes 8847360 | tf_op jit(solution)/shard_map/stack | solution.py:88
  69.6 15.4 %all-to-all-done.1 = bf16[6,128,512]{2,0,1:T(8,128)(2,1)S(1)} async-done(((bf16[6,128,512]{2,0,1:T(8,128)(2,1)}), bf16[6,128,512]{2,0,1:T(8,128)(2,1)S(1)}, u32[]{:S(2)}, u32[]{:S(2)}) %all-to-all-start.1) | async-done | bytes 786464 | tf_op jit(solution)/shard_map/all_to_all | solution.py:145
  85.5 1.1 fusion.161
  86.6 3.8 %fusion.113 = f32[2880,256]{1,0:T(8,128)S(1)} fusion(bf16[2880,768]{1,0:T(8,128)(2,1)} %bitcast.122, bf16[768,1,256]{2,1,0:T(2,128)(2,1)S(1)} %get-tuple-element.72), kind=kOutput, calls=%fused_computation.232 | convolution fusion | flops 1132462080 | bytes 7766016 | tf_op jit(solution)/shard_map/qs,sn->qn/dot_general | solution.py:152
  90.4 1.3 fusion.116
  91.9 2.4 %fusion.103 = (f32[128]{0:T(128)S(1)}, f32[128]{0:T(128)S(1)}, f32[128]{0:T(128)S(1)}, f32[128]{0:T(128)S(1)}, f32[128]{0:T(128)S(1)}, /*index=5*/f32[128]{0:T(1...) fusion(f32[6,1440,128]{2,1,0:T(8,128)S(1)} %bitcast.121, ...), kind=kOutput, calls=%fused_computation.206 | convolution fusion | flops 105429888 | bytes 5960192 | tf_op jit(solution)/shard_map/rqd,cd->rqc/dot_general | solution.py:156
  94.4 2.1 %collective-permute-start.5 = (bf16[2,1440,128]{2,1,0:T(8,128)(2,1)S(1)}, bf16[2,1440,128]{2,1,0:T(8,128)(2,1)S(1)}, u32[]{:S(2)}, u32[]{:S(2)}) collective-permute-start(bf16[2,1440,128]{2,1,0:T(8,128)(2,1)S(1)} %get-tuple-element.110), channel_id=1, source_target_pairs={{0,8},{8,16},{16,24},{24,32},{32,40},{40,48},{48,56},{56,64},{64,7... | collective-permute-start | bytes 2211848 | tf_op jit(solution)/shard_map/ppermute | solution.py:23
  96.4 2.4 %collective-permute-start.6 = (bf16[2,1440,128]{2,1,0:T(8,128)(2,1)S(1)}, bf16[2,1440,128]{2,1,0:T(8,128)(2,1)S(1)}, u32[]{:S(2)}, u32[]{:S(2)}) collective-permute-start(bf16[2,1440,128]{2,1,0:T(8,128)(2,1)S(1)} %get-tuple-element.110), channel_id=1, source_target_pairs={{8,0},{16,8},{24,16},{32,24},{40,32},{48,40},{56,48},{64,56},{72,6... | collective-permute-start | bytes 2211848 | tf_op jit(solution)/shard_map/ppermute | solution.py:24
  98.9 3.4 %fusion.106 = (f32[128]{0:T(128)S(1)}, f32[128]{0:T(128)S(1)}, f32[128]{0:T(128)S(1)}, f32[128]{0:T(128)S(1)}, f32[128]{0:T(128)S(1)}, /*index=5*/f32[128]{0:T(1...) fusion(bf16[2,1440,128]{2,1,0:T(8,128)(2,1)S(1)} %get-tuple-element.110, f32[6,8,128]{2,1,0:T(8,128)S(1)} %get-tuple-element.69, ...), kind=kLoop, calls=%fused_computation.209 | loop fusion | flops 10320768 | bytes 5190144 | tf_op jit(solution)/shard_map/reduce_sum | solution.py:166
  102.8 0.9 copy-done.3
  103.7 0.8 fusion.107
  104.6 1.3 collective-permute-start.3
  105.9 0.8 collective-permute-start.4
  106.8 8.6 %collective-permute-done.3 = f32[128,153]{0,1:T(8,128)S(1)} collective-permute-done((f32[128,153]{0,1:T(8,128)S(1)}, f32[128,153]{0,1:T(8,128)S(1)}, u32[]{:S(2)}, u32[]{:S(2)}) %collective-permute-start.3) | collective-permute-done | bytes 78368 | tf_op jit(solution)/shard_map/ppermute | solution.py:39
  115.3 0.9 collective-permute-done.4
  117.0 1.5 %fusion.15 = f32[2,1440,128]{2,1,0:T(8,128)S(1)} fusion(f32[6,1440,128]{2,1,0:T(8,128)S(1)} %maximum_convert_fusion.1, f32[6,8,128]{2,1,0:T(8,128)S(1)} %get-tuple-element.68, f32[6,8,128]{2,1,0:T(8,128)S(1)} %get-tuple-element.67, f32[128]{0:T(128)S(1)} %copy-done.15, f32[128]{0:T(128)S(1)} %copy-done.17, f32[128]{0:T(128)S(1)} %copy-done.19, ...), kind=kLoop, calls=%fused_computation.118 | loop fusion | flops 7741440 | bytes 8900608 | tf_op jit(solution)/shard_map/add | solution.py:178
  118.5 0.6 collective-permute-start.7
  119.2 2.3 %collective-permute-start.8 = (f32[128,153]{0,1:T(8,128)S(1)}, f32[128,153]{0,1:T(8,128)S(1)}, u32[]{:S(2)}, u32[]{:S(2)}) collective-permute-start(f32[128,153]{0,1:T(8,128)S(1)} %add_add_fusion.2), channel_id=1, source_target_pairs={{0,4},{1,5},{2,6},{3,7},{4,0},{5,1},{6,2},{7,3},{8,12},{9,13},{10,... | collective-permute-start | bytes 235016 | tf_op jit(solution)/shard_map/ppermute | solution.py:39
  121.4 1.0 collective-permute-start.9
  122.5 1.7 %fusion.27 = f32[2,1440,128]{2,1,0:T(8,128)S(1)} fusion(f32[2,1440,128]{2,1,0:T(8,128)S(1)} %fusion.15, f32[6,1440,128]{2,1,0:T(8,128)S(1)} %maximum_convert_fusion.1, f32[6,8,128]{2,1,0:T(8,128)S(1)} %get-tuple-element.68, f32[6,8,128]{2,1,0:T(8,128)S(1)} %get-tuple-element.67, f32[128]{0:T(128)S(1)} %get-tuple-element.83, f32[128]{0:T(128)S(1)} %get-tuple-element.84, ...), kind=kLoop, calls=%fused_computation.130 | loop fusion | flops 8478720 | bytes 8900608 | tf_op jit(solution)/shard_map/add | solution.py:178
  124.2 2.0 %collective-permute-done.8 = f32[128,153]{0,1:T(8,128)S(1)} collective-permute-done((f32[128,153]{0,1:T(8,128)S(1)}, f32[128,153]{0,1:T(8,128)S(1)}, u32[]{:S(2)}, u32[]{:S(2)}) %collective-permute-start.8) | collective-permute-done | bytes 78368 | tf_op jit(solution)/shard_map/ppermute | solution.py:39
  126.2 1.7 %collective-permute-done.9 = f32[128,153]{0,1:T(8,128)S(1)} collective-permute-done((f32[128,153]{0,1:T(8,128)S(1)}, f32[128,153]{0,1:T(8,128)S(1)}, u32[]{:S(2)}, u32[]{:S(2)}) %collective-permute-start.9) | collective-permute-done | bytes 78368 | tf_op jit(solution)/shard_map/ppermute | solution.py:39
  127.9 2.8 %collective-permute-start.10 = (f32[128,153]{0,1:T(8,128)S(1)}, f32[128,153]{0,1:T(8,128)S(1)}, u32[]{:S(2)}, u32[]{:S(2)}) collective-permute-start(f32[128,153]{0,1:T(8,128)S(1)} %add_add_fusion.1), channel_id=1, source_target_pairs={{0,32},{1,33},{2,34},{3,35},{4,36},{5,37},{6,38},{7,39},{8,40},{9,... | collective-permute-start | bytes 235016 | tf_op jit(solution)/shard_map/ppermute | solution.py:39
  130.7 1.8 %collective-permute-start.11 = (f32[128,153]{0,1:T(8,128)S(1)}, f32[128,153]{0,1:T(8,128)S(1)}, u32[]{:S(2)}, u32[]{:S(2)}) collective-permute-start(f32[128,153]{0,1:T(8,128)S(1)} %add_add_fusion.1), channel_id=1, source_target_pairs={{0,64},{1,65},{2,66},{3,67},{4,68},{5,69},{6,70},{7,71},{8,72},{9,... | collective-permute-start | bytes 235016 | tf_op jit(solution)/shard_map/ppermute | solution.py:39
  132.5 0.7 collective-permute-start.12
  133.2 2.9 %fusion.8 = bf16[2,1440,128]{2,1,0:T(8,128)(2,1)} fusion(f32[6,1440,128]{2,1,0:T(8,128)S(1)} %maximum_convert_fusion.1, f32[2,1440,128]{2,1,0:T(8,128)S(1)} %fusion.27, f32[6,8,128]{2,1,0:T(8,128)S(1)} %get-tuple-element.68, f32[6,8,128]{2,1,0:T(8,128)S(1)} %get-tuple-element.67, f32[128]{0:T(128)S(1)} %get-tuple-element.98, f32[128]{0:T(128)S(1)} %get-tuple-element.99, ...), kind=kLoop, calls=%fused_computation.111 | loop fusion | flops 9584640 | bytes 9638400 | tf_op jit(solution)/shard_map/add | solution.py:178
  136.7 1.8 %collective-permute-done.12 = f32[128,153]{0,1:T(8,128)S(1)} collective-permute-done((f32[128,153]{0,1:T(8,128)S(1)}, f32[128,153]{0,1:T(8,128)S(1)}, u32[]{:S(2)}, u32[]{:S(2)}) %collective-permute-start.12) | collective-permute-done | bytes 78368 | tf_op jit(solution)/shard_map/ppermute | solution.py:39
  138.5 0.7 collective-permute-start.13
  139.2 4.2 %collective-permute-done.13 = f32[128,153]{0,1:T(8,128)S(1)} collective-permute-done((f32[128,153]{0,1:T(8,128)S(1)}, f32[128,153]{0,1:T(8,128)S(1)}, u32[]{:S(2)}, u32[]{:S(2)}) %collective-permute-start.13) | collective-permute-done | bytes 78368 | tf_op jit(solution)/shard_map/ppermute | solution.py:39
  143.4 0.6 slice.559
  144.0 0.7 copy.19
  (99 shorter events, 4.6 us)
Async XLA Ops:
  0.6 91.2 %copy-start = (bf16[128,128]{1,0:T(8,128)(2,1)S(1)}, bf16[128,128]{1,0:T(8,128)(2,1)}, u32[]{:S(2)}) copy-start(bf16[128,128]{1,0:T(8,128)(2,1)} %param.15) | copy-start | bytes 98308
  0.6 24.8 %collective-permute-start = (bf16[2,1440,128]{2,1,0:T(8,128)(2,1)}, bf16[2,1440,128]{2,1,0:T(8,128)(2,1)S(1)}, u32[]{:S(2)}, u32[]{:S(2)}) collective-permute-start(bf16[2,1440,128]{2,1,0:T(8,128)(2,1)} %bitcast.129), channel_id=1, source_target_pairs={{0,8},{8,16},{16,24},{24,32},{32,40},{40,48},{48,56},{56,64},{64,7... | collective-permute-start | bytes 2211848 | tf_op jit(solution)/shard_map/ppermute | solution.py:23
  5.2 20.3 %collective-permute-start.1 = (bf16[2,1440,128]{2,1,0:T(8,128)(2,1)}, bf16[2,1440,128]{2,1,0:T(8,128)(2,1)}, u32[]{:S(2)}, u32[]{:S(2)}) collective-permute-start(bf16[2,1440,128]{2,1,0:T(8,128)(2,1)} %bitcast.130), channel_id=1, source_target_pairs={{8,0},{16,8},{24,16},{32,24},{40,32},{48,40},{56,48},{64,56},{72,6... | collective-permute-start | bytes 2211848 | tf_op jit(solution)/shard_map/ppermute | solution.py:24
  11.2 7.5 %copy-start.9 = (s32[768]{0:T(1024)S(1)}, s32[768]{0:T(1024)}, u32[]{:S(2)}) copy-start(s32[768]{0:T(1024)} %param.11) | copy-start | bytes 9220
  11.2 8.1 %copy-start.10 = (f32[128,25]{0,1:T(8,128)S(1)}, f32[128,25]{0,1:T(8,128)}, u32[]{:S(2)}) copy-start(f32[128,25]{0,1:T(8,128)} %param.14) | copy-start | bytes 38404
  11.2 8.7 %copy-start.28 = (s32[48]{0:T(128)S(1)}, s32[48]{0:T(128)}, u32[]{:S(2)}) copy-start(s32[48]{0:T(128)} %param.12) | copy-start | bytes 580
  11.2 43.5 %all-to-all-start = ((bf16[8,200,768]{2,1,0:T(8,128)(2,1)}), bf16[8,200,768]{2,1,0:T(8,128)(2,1)S(1)}, u32[]{:S(2)}, u32[]{:S(2)}) async-start(bf16[8,200,768]{2,1,0:T(8,128)(2,1)} %pad_maximum_fusion.1), calls=%async_computation | async-start | bytes 4915200 | tf_op jit(solution)/shard_map/all_to_all | solution.py:116
  20.1 6.9 %copy-start.20 = (f32[128]{0:T(128)}, f32[128]{0:T(128)S(1)}, u32[]{:S(2)}) copy-start(f32[128]{0:T(128)S(1)} %get-tuple-element.94) | copy-start | bytes 1540
  20.1 6.9 %copy-start.22 = (f32[128]{0:T(128)}, f32[128]{0:T(128)S(1)}, u32[]{:S(2)}) copy-start(f32[128]{0:T(128)S(1)} %get-tuple-element.95) | copy-start | bytes 1540
  20.1 6.9 %copy-start.24 = (f32[128]{0:T(128)}, f32[128]{0:T(128)S(1)}, u32[]{:S(2)}) copy-start(f32[128]{0:T(128)S(1)} %get-tuple-element.96) | copy-start | bytes 1540
  20.1 6.9 %copy-start.26 = (f32[128]{0:T(128)}, f32[128]{0:T(128)S(1)}, u32[]{:S(2)}) copy-start(f32[128]{0:T(128)S(1)} %get-tuple-element.97) | copy-start | bytes 1540
  21.4 4.1 %copy-start.6 = (bf16[2,128,1440]{1,2,0:T(8,128)(2,1)S(1)}, bf16[2,128,1440]{1,2,0:T(8,128)(2,1)}, u32[]{:S(2)}) copy-start(bf16[2,128,1440]{1,2,0:T(8,128)(2,1)} %param.13) | copy-start | bytes 2211844
  25.4 3.5 %copy-start.11 = (f32[128]{0:T(128)S(1)}, f32[128]{0:T(128)}, u32[]{:S(2)}) copy-start(f32[128]{0:T(128)} %get-tuple-element.88) | copy-start | bytes 1540
  25.4 3.5 %copy-start.12 = (f32[128]{0:T(128)S(1)}, f32[128]{0:T(128)}, u32[]{:S(2)}) copy-start(f32[128]{0:T(128)} %get-tuple-element.89) | copy-start | bytes 1540
  25.4 3.5 %copy-start.13 = (f32[128]{0:T(128)S(1)}, f32[128]{0:T(128)}, u32[]{:S(2)}) copy-start(f32[128]{0:T(128)} %get-tuple-element.90) | copy-start | bytes 1540
  25.4 3.5 %copy-start.14 = (f32[128]{0:T(128)S(1)}, f32[128]{0:T(128)}, u32[]{:S(2)}) copy-start(f32[128]{0:T(128)} %get-tuple-element.75) | copy-start | bytes 1540
  25.4 3.5 %copy-start.15 = (f32[128]{0:T(128)S(1)}, f32[128]{0:T(128)}, u32[]{:S(2)}) copy-start(f32[128]{0:T(128)} %get-tuple-element.91) | copy-start | bytes 1540
  25.5 3.5 %copy-start.16 = (f32[128]{0:T(128)S(1)}, f32[128]{0:T(128)}, u32[]{:S(2)}) copy-start(f32[128]{0:T(128)} %get-tuple-element.92) | copy-start | bytes 1540
  25.5 3.5 %copy-start.18 = (f32[128]{0:T(128)S(1)}, f32[128]{0:T(128)}, u32[]{:S(2)}) copy-start(f32[128]{0:T(128)} %get-tuple-element.93) | copy-start | bytes 1540
  26.9 2.0 %copy-start.1 = (f32[6,1440,128]{2,1,0:T(8,128)}, f32[6,1440,128]{2,1,0:T(8,128)S(1)}, u32[]{:S(2)}) copy-start(f32[6,1440,128]{2,1,0:T(8,128)S(1)} %maximum_convert_fusion) | copy-start | bytes 13271044
  60.5 5.1 %copy-start.7 = (f32[36,768]{1,0:T(8,128)S(1)}, f32[36,768]{1,0:T(8,128)}, u32[]{:S(2)}) copy-start(f32[36,768]{1,0:T(8,128)} %get-tuple-element.102) | copy-start | bytes 331780
  60.5 5.1 %copy-start.8 = (f32[36,768]{1,0:T(8,128)S(1)}, f32[36,768]{1,0:T(8,128)}, u32[]{:S(2)}) copy-start(f32[36,768]{1,0:T(8,128)} %get-tuple-element.103) | copy-start | bytes 331780
  60.5 24.5 %all-to-all-start.1 = ((bf16[6,128,512]{2,0,1:T(8,128)(2,1)}), bf16[6,128,512]{2,0,1:T(8,128)(2,1)S(1)}, u32[]{:S(2)}, u32[]{:S(2)}) async-start(bf16[6,128,512]{2,0,1:T(8,128)(2,1)} %copy.18), calls=%async_computation.1 | async-start | bytes 2097152 | tf_op jit(solution)/shard_map/all_to_all | solution.py:145
  86.6 3.8 %copy-start.2 = (bf16[2,36,40,768]{3,2,1,0:T(8,128)(2,1)S(1)}, bf16[2,36,40,768]{3,2,1,0:T(8,128)(2,1)}, u32[]{:S(2)}) copy-start(bf16[2,36,40,768]{3,2,1,0:T(8,128)(2,1)} %pad_maximum_fusion) | copy-start | bytes 13271044
  86.6 5.3 %slice-start = ((s8[4423680]{0:T(1024)(128)(4,1)}), s8[4194304]{0:T(1024)(128)(4,1)S(1)}, s32[]{:S(2)}) async-start(s8[4423680]{0:T(1024)(128)(4,1)} %bitcast.120), calls=%async_computation.2 | async-start | bytes 8388608
  90.4 1.5 %slice-start.1 = ((s8[4423680]{0:T(1024)(128)(4,1)}), s8[229376]{0:T(1024)(128)(4,1)S(1)}, s32[]{:S(2)}) async-start(s8[4423680]{0:T(1024)(128)(4,1)} %bitcast.120), calls=%async_computation.3 | async-start | bytes 458752
  94.3 8.0 %copy-start.5 = (bf16[2,1440,128]{2,1,0:T(8,128)(2,1)S(1)}, bf16[2,1440,128]{2,1,0:T(8,128)(2,1)}, u32[]{:S(2)}) copy-start(bf16[2,1440,128]{2,1,0:T(8,128)(2,1)} %get-tuple-element.14) | copy-start | bytes 2211844
  94.4 22.0 %collective-permute-start.5 = (bf16[2,1440,128]{2,1,0:T(8,128)(2,1)S(1)}, bf16[2,1440,128]{2,1,0:T(8,128)(2,1)S(1)}, u32[]{:S(2)}, u32[]{:S(2)}) collective-permute-start(bf16[2,1440,128]{2,1,0:T(8,128)(2,1)S(1)} %get-tuple-element.110), channel_id=1, source_target_pairs={{0,8},{8,16},{16,24},{24,32},{32,40},{40,48},{48,56},{56,64},{64,7... | collective-permute-start | bytes 2211848 | tf_op jit(solution)/shard_map/ppermute | solution.py:23
  96.4 19.9 %collective-permute-start.6 = (bf16[2,1440,128]{2,1,0:T(8,128)(2,1)S(1)}, bf16[2,1440,128]{2,1,0:T(8,128)(2,1)S(1)}, u32[]{:S(2)}, u32[]{:S(2)}) collective-permute-start(bf16[2,1440,128]{2,1,0:T(8,128)(2,1)S(1)} %get-tuple-element.110), channel_id=1, source_target_pairs={{8,0},{16,8},{24,16},{32,24},{40,32},{48,40},{56,48},{64,56},{72,6... | collective-permute-start | bytes 2211848 | tf_op jit(solution)/shard_map/ppermute | solution.py:24
  98.9 3.9 %copy-start.4 = (f32[2,1440,128]{2,1,0:T(8,128)S(1)}, f32[2,1440,128]{2,1,0:T(8,128)}, u32[]{:S(2)}) copy-start(f32[2,1440,128]{2,1,0:T(8,128)} %get-tuple-element.66) | copy-start | bytes 4423684
  102.3 1.4 copy-start.3
  104.6 2.2 %collective-permute-start.2 = (f32[128,153]{0,1:T(8,128)S(1)}, f32[128,153]{0,1:T(8,128)S(1)}, u32[]{:S(2)}, u32[]{:S(2)}) collective-permute-start(f32[128,153]{0,1:T(8,128)S(1)} %concatenate.70), channel_id=1, source_target_pairs={{0,8},{1,9},{2,10},{3,11},{4,12},{5,13},{6,14},{7,15},{8,0},{9,1},... | collective-permute-start | bytes 235016 | tf_op jit(solution)/shard_map/ppermute | solution.py:39
  104.6 10.7 %collective-permute-start.3 = (f32[128,153]{0,1:T(8,128)S(1)}, f32[128,153]{0,1:T(8,128)S(1)}, u32[]{:S(2)}, u32[]{:S(2)}) collective-permute-start(f32[128,153]{0,1:T(8,128)S(1)} %concatenate.70), channel_id=1, source_target_pairs={{0,16},{1,17},{2,18},{3,19},{4,20},{5,21},{6,22},{7,23},{8,24},{9,... | collective-permute-start | bytes 235016 | tf_op jit(solution)/shard_map/ppermute | solution.py:39
  105.9 10.3 %collective-permute-start.4 = (f32[128,153]{0,1:T(8,128)S(1)}, f32[128,153]{0,1:T(8,128)S(1)}, u32[]{:S(2)}, u32[]{:S(2)}) collective-permute-start(f32[128,153]{0,1:T(8,128)S(1)} %concatenate.70), channel_id=1, source_target_pairs={{0,24},{1,25},{2,26},{3,27},{4,28},{5,29},{6,30},{7,31},{8,16},{9,... | collective-permute-start | bytes 235016 | tf_op jit(solution)/shard_map/ppermute | solution.py:39
  116.3 0.7 copy-start.17
  116.3 0.7 copy-start.19
  116.3 0.7 copy-start.21
  116.3 0.7 copy-start.23
  116.3 0.6 copy-start.25
  116.3 0.6 copy-start.27
  118.5 5.6 %collective-permute-start.7 = (f32[128,153]{0,1:T(8,128)S(1)}, f32[128,153]{0,1:T(8,128)S(1)}, u32[]{:S(2)}, u32[]{:S(2)}) collective-permute-start(f32[128,153]{0,1:T(8,128)S(1)} %add_add_fusion.2), channel_id=1, source_target_pairs={{0,2},{1,3},{2,0},{3,1},{4,6},{5,7},{6,4},{7,5},{8,10},{9,11},{10,... | collective-permute-start | bytes 235016 | tf_op jit(solution)/shard_map/ppermute | solution.py:39
  119.2 7.0 %collective-permute-start.8 = (f32[128,153]{0,1:T(8,128)S(1)}, f32[128,153]{0,1:T(8,128)S(1)}, u32[]{:S(2)}, u32[]{:S(2)}) collective-permute-start(f32[128,153]{0,1:T(8,128)S(1)} %add_add_fusion.2), channel_id=1, source_target_pairs={{0,4},{1,5},{2,6},{3,7},{4,0},{5,1},{6,2},{7,3},{8,12},{9,13},{10,... | collective-permute-start | bytes 235016 | tf_op jit(solution)/shard_map/ppermute | solution.py:39
  121.4 6.5 %collective-permute-start.9 = (f32[128,153]{0,1:T(8,128)S(1)}, f32[128,153]{0,1:T(8,128)S(1)}, u32[]{:S(2)}, u32[]{:S(2)}) collective-permute-start(f32[128,153]{0,1:T(8,128)S(1)} %add_add_fusion.2), channel_id=1, source_target_pairs={{0,6},{1,7},{2,4},{3,5},{4,2},{5,3},{6,0},{7,1},{8,14},{9,15},{10,... | collective-permute-start | bytes 235016 | tf_op jit(solution)/shard_map/ppermute | solution.py:39
  127.9 8.1 %collective-permute-start.10 = (f32[128,153]{0,1:T(8,128)S(1)}, f32[128,153]{0,1:T(8,128)S(1)}, u32[]{:S(2)}, u32[]{:S(2)}) collective-permute-start(f32[128,153]{0,1:T(8,128)S(1)} %add_add_fusion.1), channel_id=1, source_target_pairs={{0,32},{1,33},{2,34},{3,35},{4,36},{5,37},{6,38},{7,39},{8,40},{9,... | collective-permute-start | bytes 235016 | tf_op jit(solution)/shard_map/ppermute | solution.py:39
  130.7 5.9 %collective-permute-start.11 = (f32[128,153]{0,1:T(8,128)S(1)}, f32[128,153]{0,1:T(8,128)S(1)}, u32[]{:S(2)}, u32[]{:S(2)}) collective-permute-start(f32[128,153]{0,1:T(8,128)S(1)} %add_add_fusion.1), channel_id=1, source_target_pairs={{0,64},{1,65},{2,66},{3,67},{4,68},{5,69},{6,70},{7,71},{8,72},{9,... | collective-permute-start | bytes 235016 | tf_op jit(solution)/shard_map/ppermute | solution.py:39
  132.5 6.0 %collective-permute-start.12 = (f32[128,153]{0,1:T(8,128)S(1)}, f32[128,153]{0,1:T(8,128)S(1)}, u32[]{:S(2)}, u32[]{:S(2)}) collective-permute-start(f32[128,153]{0,1:T(8,128)S(1)} %add_add_fusion.1), channel_id=1, source_target_pairs={{0,96},{1,97},{2,98},{3,99},{4,100},{5,101},{6,102},{7,103},{8,104... | collective-permute-start | bytes 235016 | tf_op jit(solution)/shard_map/ppermute | solution.py:39
  138.5 4.9 %collective-permute-start.13 = (f32[128,153]{0,1:T(8,128)S(1)}, f32[128,153]{0,1:T(8,128)S(1)}, u32[]{:S(2)}, u32[]{:S(2)}) collective-permute-start(f32[128,153]{0,1:T(8,128)S(1)} %add_add_fusion), channel_id=1, source_target_pairs={{0,1},{1,0},{2,3},{3,2},{4,5},{5,4},{6,7},{7,6},{8,9},{9,8},{10,11... | collective-permute-start | bytes 235016 | tf_op jit(solution)/shard_map/ppermute | solution.py:39
